TPU v7x, 512 devices: a whole 4x4x16 slice. The times are simulated.
512 devices in a mesh: path: 64 (over x, z_hi, y, core), trade: 8 (over z_lo).
Axes of the slice: x: 4, y: 4, z: 16 (z_hi: 2, z_lo: 8; z = z_hi * 8 + z_lo), core: 2. Of those that a mesh axis runs over, the one named last changes fastest.
Arguments:
- drivers: bfloat16 [8192, 4096], P('path'), may hold values from -5 to 5
- loadings: bfloat16 [4096, 8192], P('path', 'trade'), may hold values from -0.09375 to 0.09375
- start_state: bfloat16 [8192, 8192], P('path', 'trade'), may hold values from -4 to 4
- coeffs: bfloat16 [8192, 64], P('trade'), may hold values from -1 to 1
- trade_col: int32 [8192], P('trade'), may hold values from 0 to 8191, as said below
- trade_ns: int32 [8192], P('trade'), may hold values from 0 to 2047, as said below
- ns_cp: int32 [2048], P('trade'), may hold values from 0 to 255
Outputs:
- cp_exposure: float32 [256, 8192], P('trade', 'path')
Inputs may be any that keep to these rules, and one draw needn't show every extreme that they name: `trade_ns`: each netting set holds 1 to 32 trades, at least one exactly 32. `trade_col`: the trades of one index of trade have exactly 128 trades reading from each of the aligned blocks of 1024 factors held by one index of trade.
All inputs are finite; a program needn't handle non-finite values.
Results may differ from a plain program's by a relative error of at most 0.0059.
The roundings to bfloat16 on the way count: a program that leaves them out, or rounds other values in their place, can miss the bound.
Values may be sent and summed in bfloat16 or wider, within the bound.
No kernel may reach another device: no remote copies, remote signals or barrier semaphores. Data moves between devices by JAX's collectives and lax.ppermute only.
A program may use at most 64 MiB of HBM per device.

v0:
```python
import jax
import jax.numpy as jnp
from jax import lax
from jax.sharding import PartitionSpec as P

CP_DEV = 32


def valuation(chosen, coeffs):
    count = chosen.shape[1]
    rows = chosen.shape[0]
    terms = coeffs.shape[1]
    block = min(128, count)
    blocks = count // block
    orders = jnp.arange(terms, dtype=jnp.float32)

    def one_block(pair):
        factor_part, coeff_part = pair
        theta = jnp.arccos(jnp.tanh(factor_part.astype(jnp.float32) * 0.5))
        basis = jnp.cos(theta[:, :, None] * orders[None, None, :])
        return jnp.einsum(
            "ptk,tk->pt", basis, coeff_part.astype(jnp.float32), precision=lax.Precision.HIGHEST
        )

    factor_blocks = chosen.reshape(rows, blocks, block).transpose(1, 0, 2)
    coeff_blocks = coeffs.reshape(blocks, block, terms)
    values = lax.map(one_block, (factor_blocks, coeff_blocks))
    return values.transpose(1, 0, 2).reshape(rows, count).astype(jnp.bfloat16)


def per_device(drivers, loadings, start_state, coeffs, trade_col, trade_ns, ns_cp):
    owners = lax.axis_size("trade")
    moved = jnp.dot(
        drivers,
        lax.all_gather(loadings, "path", axis=0, tiled=True),
        preferred_element_type=jnp.float32,
    )
    factors = (start_state.astype(jnp.float32) + moved).astype(jnp.bfloat16)
    whole = lax.all_gather(factors, "trade", axis=1, tiled=True)
    chosen = jnp.take(whole, trade_col, axis=1)
    values = valuation(chosen, coeffs)
    total_sets = ns_cp.shape[0] * owners
    net_table = (trade_ns[:, None] == jnp.arange(total_sets, dtype=jnp.int32)[None, :]).astype(
        jnp.bfloat16
    )
    netting = jnp.dot(values, net_table, preferred_element_type=jnp.float32)
    shares = lax.psum_scatter(netting, "trade", scatter_dimension=1, tiled=True)
    positive = jnp.maximum(shares, 0.0).astype(jnp.bfloat16)
    cp_table = (ns_cp[:, None] == jnp.arange(CP_DEV * owners, dtype=jnp.int32)[None, :]).astype(
        jnp.bfloat16
    )
    partial_cp = jnp.dot(positive, cp_table, preferred_element_type=jnp.float32)
    exposure = lax.psum_scatter(partial_cp, "trade", scatter_dimension=1, tiled=True).T
    return exposure


def solution(mesh):
    return jax.shard_map(
        per_device,
        mesh=mesh,
        in_specs=(
            P("path", None),
            P("path", "trade"),
            P("path", "trade"),
            P("trade", None),
            P("trade"),
            P("trade"),
            P("trade"),
        ),
        out_specs=P("trade", "path"),
        check_vma=False,
    )
```

profile of v0, /device:TPU:6, one launch (start us, length us, event | category | flops | bytes accessed | tf_op | source)
XLA Modules:
  0.0 521.5 jit_solution(2517889155304148091)
XLA Ops:
  6.5 0.7 all-gather.3.cloned.1.call-update
  7.3 0.0 all-gather.5.cloned.1.call-start
  7.3 172.2 %all-gather.3.cloned.1.call-done = bf16[4096,1024]{1,0:T(8,128)(2,1)} async-done(((bf16[64,1024]{1,0:T(8,128)(2,1)}), bf16[4096,1024]{1,0:T(8,128)(2,1)}) %all-gather.3.cloned.1.call-update) | async-done | bytes 8388624 | tf_op jit(solution)/shard_map/all_gather | solution.py:35
  179.5 5.4 %fusion.10 = bf16[128,1024]{1,0:T(8,128)(2,1)} fusion(bf16[128,4096]{1,0:T(8,128)(2,1)S(1)} %copy-done, bf16[4096,1024]{1,0:T(8,128)(2,1)} %all-gather.3.cloned.1.call-done, bf16[128,1024]{1,0:T(8,128)(2,1)} %param.11), kind=kOutput, calls=%fused_computation.18 | convolution fusion | flops 1074135040 | bytes 9961472 | tf_op jit(solution)/shard_map/dot_general | solution.py:33
  184.9 0.0 reduce-scatter.3.cloned.1.call-start
  185.0 0.8 copy.15
  185.9 68.6 %all-gather.5.cloned.1.call-done = bf16[128,8192]{1,0:T(8,128)(2,1)} async-done(((bf16[128,1024]{1,0:T(8,128)(2,1)}), bf16[128,8192]{1,0:T(8,128)(2,1)}) %all-gather.5.cloned.1.call-update) | async-done | bytes 2097168 | tf_op jit(solution)/shard_map/all_gather | solution.py:39
  254.5 3.2 copy.16
  257.7 3.2 gather_fusion
  260.9 0.2 copy.17
  261.2 125.7 %while.11 = (s32[]{:T(128)}, bf16[8,128,128]{1,2,0:T(8,128)(2,1)}, bf16[8,128,64]{2,1,0:T(8,128)(2,1)}, bf16[8,128,128]{2,1,0:T(8,128)(2,1)S(1)}, s32[]{:T(128)}) while((s32[]{:T(128)}, bf16[8,128,128]{1,2,0:T(8,128)(2,1)}, bf16[8,128,64]{2,1,0:T(8,128)(2,1)}, bf16[8,128,128]{2,1,0:T(8,128)(2,1)S(1)}, s32[]{:T(128)}) %tuple.32), condition=%wide.region_1.2_spmd.clone, body=%wide.region_0.1_spmd.clone.sunk | while | flops 3219458 | bytes 475717 | solution.py:27
  261.2 0.8 bitcast_convert_fusion.2
  261.9 0.1 copy.31
  262.0 0.2 bitcast_atan2_fusion.2
  262.2 14.0 %fusion.20 = bf16[128,128]{0,1:T(8,128)(2,1)S(1)} fusion(f32[128,64]{0,1:T(8,128)S(1)} %copy.31, f32[128,128]{1,0:T(8,128)S(1)} %bitcast_atan2_fusion.2), kind=kLoop, calls=%fused_computation.6.clone.1 | loop fusion | flops 3129344 | bytes 131072 | tf_op jit(solution)/shard_map/while/body/eval_jaxpr/ptk,tk->pt/dot_general | solution.py:21
  276.1 0.1 copy.32
  276.3 0.6 constant_dynamic-update-slice_fusion.2
  276.9 0.8 bitcast_convert_fusion.2
  277.6 0.1 copy.31
  277.7 0.2 bitcast_atan2_fusion.2
  277.9 14.0 %fusion.20 = bf16[128,128]{0,1:T(8,128)(2,1)S(1)} fusion(f32[128,64]{0,1:T(8,128)S(1)} %copy.31, f32[128,128]{1,0:T(8,128)S(1)} %bitcast_atan2_fusion.2), kind=kLoop, calls=%fused_computation.6.clone.1 | loop fusion | flops 3129344 | bytes 131072 | tf_op jit(solution)/shard_map/while/body/eval_jaxpr/ptk,tk->pt/dot_general | solution.py:21
  291.9 0.1 copy.32
  292.0 0.6 constant_dynamic-update-slice_fusion.2
  292.6 0.8 bitcast_convert_fusion.2
  293.4 0.1 copy.31
  293.4 0.2 bitcast_atan2_fusion.2
  293.6 14.0 %fusion.20 = bf16[128,128]{0,1:T(8,128)(2,1)S(1)} fusion(f32[128,64]{0,1:T(8,128)S(1)} %copy.31, f32[128,128]{1,0:T(8,128)S(1)} %bitcast_atan2_fusion.2), kind=kLoop, calls=%fused_computation.6.clone.1 | loop fusion | flops 3129344 | bytes 131072 | tf_op jit(solution)/shard_map/while/body/eval_jaxpr/ptk,tk->pt/dot_general | solution.py:21
  307.6 0.1 copy.32
  307.7 0.6 constant_dynamic-update-slice_fusion.2
  308.3 0.8 bitcast_convert_fusion.2
  309.1 0.1 copy.31
  309.1 0.2 bitcast_atan2_fusion.2
  309.3 14.0 %fusion.20 = bf16[128,128]{0,1:T(8,128)(2,1)S(1)} fusion(f32[128,64]{0,1:T(8,128)S(1)} %copy.31, f32[128,128]{1,0:T(8,128)S(1)} %bitcast_atan2_fusion.2), kind=kLoop, calls=%fused_computation.6.clone.1 | loop fusion | flops 3129344 | bytes 131072 | tf_op jit(solution)/shard_map/while/body/eval_jaxpr/ptk,tk->pt/dot_general | solution.py:21
  323.3 0.1 copy.32
  323.4 0.6 constant_dynamic-update-slice_fusion.2
  324.0 0.8 bitcast_convert_fusion.2
  324.8 0.1 copy.31
  324.9 0.2 bitcast_atan2_fusion.2
  325.0 14.0 %fusion.20 = bf16[128,128]{0,1:T(8,128)(2,1)S(1)} fusion(f32[128,64]{0,1:T(8,128)S(1)} %copy.31, f32[128,128]{1,0:T(8,128)S(1)} %bitcast_atan2_fusion.2), kind=kLoop, calls=%fused_computation.6.clone.1 | loop fusion | flops 3129344 | bytes 131072 | tf_op jit(solution)/shard_map/while/body/eval_jaxpr/ptk,tk->pt/dot_general | solution.py:21
  339.0 0.1 copy.32
  339.1 0.6 constant_dynamic-update-slice_fusion.2
  339.7 0.8 bitcast_convert_fusion.2
  340.5 0.1 copy.31
  340.6 0.2 bitcast_atan2_fusion.2
  340.7 14.0 %fusion.20 = bf16[128,128]{0,1:T(8,128)(2,1)S(1)} fusion(f32[128,64]{0,1:T(8,128)S(1)} %copy.31, f32[128,128]{1,0:T(8,128)S(1)} %bitcast_atan2_fusion.2), kind=kLoop, calls=%fused_computation.6.clone.1 | loop fusion | flops 3129344 | bytes 131072 | tf_op jit(solution)/shard_map/while/body/eval_jaxpr/ptk,tk->pt/dot_general | solution.py:21
  354.7 0.1 copy.32
  354.8 0.6 constant_dynamic-update-slice_fusion.2
  355.4 0.8 bitcast_convert_fusion.2
  356.2 0.1 copy.31
  356.3 0.2 bitcast_atan2_fusion.2
  356.5 14.0 %fusion.20 = bf16[128,128]{0,1:T(8,128)(2,1)S(1)} fusion(f32[128,64]{0,1:T(8,128)S(1)} %copy.31, f32[128,128]{1,0:T(8,128)S(1)} %bitcast_atan2_fusion.2), kind=kLoop, calls=%fused_computation.6.clone.1 | loop fusion | flops 3129344 | bytes 131072 | tf_op jit(solution)/shard_map/while/body/eval_jaxpr/ptk,tk->pt/dot_general | solution.py:21
  370.4 0.1 copy.32
  370.5 0.6 constant_dynamic-update-slice_fusion.2
  371.2 0.8 bitcast_convert_fusion.2
  371.9 0.1 copy.31
  372.0 0.2 bitcast_atan2_fusion.2
  372.2 14.0 %fusion.20 = bf16[128,128]{0,1:T(8,128)(2,1)S(1)} fusion(f32[128,64]{0,1:T(8,128)S(1)} %copy.31, f32[128,128]{1,0:T(8,128)S(1)} %bitcast_atan2_fusion.2), kind=kLoop, calls=%fused_computation.6.clone.1 | loop fusion | flops 3129344 | bytes 131072 | tf_op jit(solution)/shard_map/while/body/eval_jaxpr/ptk,tk->pt/dot_general | solution.py:21
  386.1 0.1 copy.32
  386.3 0.6 constant_dynamic-update-slice_fusion.2
  386.9 3.8 fusion.8
  390.7 0.0 reduce-scatter.5.cloned.1.call-start
  390.8 64.2 %reduce-scatter.3.cloned.1.call-done = f32[128,256]{1,0:T(8,128)} async-done(((f32[128,2048]{1,0:T(8,128)}), f32[128,256]{1,0:T(8,128)}) %reduce-scatter.3.cloned.1.call-update) | async-done | bytes 131088 | tf_op jit(solution)/shard_map/reduce_scatter | solution.py:47
  455.0 1.9 fusion.11
  456.9 58.1 %reduce-scatter.5.cloned.1.call-done = f32[128,32]{0,1:T(8,128)} async-done(((f32[128,256]{0,1:T(8,128)}), f32[128,32]{0,1:T(8,128)}) %reduce-scatter.5.cloned.1.call-update) | async-done | bytes 16400 | tf_op jit(solution)/shard_map/reduce_scatter | solution.py:53
  (18 shorter events, 0.1 us)
Async XLA Ops:
  6.5 173.0 %copy-start = (bf16[128,4096]{1,0:T(8,128)(2,1)S(1)}, bf16[128,4096]{1,0:T(8,128)(2,1)}, u32[]{:S(2)}) copy-start(bf16[128,4096]{1,0:T(8,128)(2,1)} %param.9) | copy-start | bytes 3145732
  6.5 173.0 %all-gather.3.cloned.1.call-start = ((), (), s32[]{:S(2)}) async-start(), calls=%async_computation.2 | async-start | bytes 8519680 | tf_op jit(solution)/shard_map/all_gather | solution.py:35
  7.3 177.7 %copy-start.1 = (bf16[1024,64]{0,1:T(8,128)(2,1)S(1)}, bf16[1024,64]{0,1:T(8,128)(2,1)}, u32[]{:S(2)}) copy-start(bf16[1024,64]{0,1:T(8,128)(2,1)} %param.12) | copy-start | bytes 393220
  7.3 178.6 %copy-start.2 = (s32[1024]{0:T(1024)S(1)}, s32[1024]{0:T(1024)}, u32[]{:S(2)}) copy-start(s32[1024]{0:T(1024)} %param.13) | copy-start | bytes 12292
  7.3 247.2 %all-gather.5.cloned.1.call-start = ((), (), s32[]{:S(2)}) async-start(), calls=%async_computation.3 | async-start | bytes 2359296 | tf_op jit(solution)/shard_map/all_gather | solution.py:39
  184.9 270.1 %reduce-scatter.3.cloned.1.call-start = ((), (), s32[]{:S(2)}) async-start(), calls=%async_computation.4 | async-start | bytes 1179648 | tf_op jit(solution)/shard_map/reduce_scatter | solution.py:47
  261.1 125.8 %copy-start.4 = (s32[1024]{0:T(1024)S(1)}, s32[1024]{0:T(1024)}, u32[]{:S(2)}) copy-start(s32[1024]{0:T(1024)} %param.14) | copy-start | bytes 12292
  261.1 193.9 %copy-start.3 = (s32[256]{0:T(256)S(1)}, s32[256]{0:T(256)}, u32[]{:S(2)}) copy-start(s32[256]{0:T(256)} %param.15) | copy-start | bytes 3076
  390.7 124.3 %reduce-scatter.5.cloned.1.call-start = ((), (), s32[]{:S(2)}) async-start(), calls=%async_computation.5 | async-start | bytes 147456 | tf_op jit(solution)/shard_map/reduce_scatter | solution.py:53
Sparse Core Ops, SparseCore 0:
  11.8 167.7 all-gather.2
  185.1 69.3 all-gather.4
  390.8 64.1 reduce-scatter.2
  457.6 57.2 reduce-scatter.4
where the time goes:
time: 522 us
  waiting for transfers between devices  364 us (70%)
  other arithmetic  119 us (23%)
  local copies, waits for them, and re-layouts  13.8 us (3%)
  between operations  13.2 us (3%)
  matrix products  11.1 us (2%)
    all_gather x1, waiting for transfers between devices, per_device(): lax.all_gather(loadings, 'path', axis=0, tiled=True)  172 us
    dot_general x8, other arithmetic, one_block(): jnp.einsum('ptk,tk->pt', basis, coeff_part.astype(jnp.float32), precision...  112 us
    all_gather x1, waiting for transfers between devices, per_device(): whole = lax.all_gather(factors, 'trade', axis=1, tiled=True)  68.6 us
    reduce_scatter x1, waiting for transfers between devices, per_device(): shares = lax.psum_scatter(netting, 'trade', scatter_dimension=1, tiled=True)  64.2 us
    reduce_scatter x1, waiting for transfers between devices, per_device(): lax.psum_scatter(partial_cp, 'trade', scatter_dimension=1, tiled=True)  58.1 us
  transfers between devices with their start and end apart: 4, of which 4 were waited for; matrix products, arithmetic and copies ran while one was open for 0% of the time, Pallas kernels for 0%

commit v1 on v0

v1 whole, which is shorter than its diff:
```python
import jax
import jax.numpy as jnp
from jax import lax
from jax.sharding import PartitionSpec as P

CP_DEV = 32


def clenshaw(chosen, coeffs_t):
    x = jnp.tanh(chosen.astype(jnp.float32) * 0.5)
    twice = x + x
    terms = coeffs_t.shape[0]
    b1 = jnp.zeros_like(x)
    b2 = jnp.zeros_like(x)
    for k in range(terms - 1, 0, -1):
        b1, b2 = coeffs_t[k][None, :] + twice * b1 - b2, b1
    return (coeffs_t[0][None, :] + x * b1 - b2).astype(jnp.bfloat16)


def regroup(trade_col, width, owners):
    count = trade_col.shape[0]
    per = count // owners
    block = trade_col // width
    onehot = (block[:, None] == jnp.arange(owners, dtype=jnp.int32)[None, :]).astype(jnp.bfloat16)
    lower = (
        jnp.arange(count, dtype=jnp.int32)[:, None] >= jnp.arange(count, dtype=jnp.int32)[None, :]
    ).astype(jnp.bfloat16)
    running = jnp.dot(lower, onehot, preferred_element_type=jnp.float32)
    rank = jnp.sum(running * onehot.astype(jnp.float32), axis=1).astype(jnp.int32) - 1
    slot = block * per + rank
    return (slot[:, None] == jnp.arange(count, dtype=jnp.int32)[None, :]).astype(jnp.float32)


def per_device(drivers, loadings, start_state, coeffs, trade_col, trade_ns, ns_cp):
    owners = lax.axis_size("trade")
    width = start_state.shape[1]
    count, terms = coeffs.shape
    per = count // owners

    place = regroup(trade_col, width, owners)
    offset = (trade_col % width).astype(jnp.float32)
    table = jnp.concatenate(
        [coeffs.astype(jnp.float32), offset[:, None], trade_ns.astype(jnp.float32)[:, None]], axis=1
    )
    sent = jnp.dot(place.T, table, precision=lax.Precision.HIGHEST)
    got = lax.all_to_all(sent.reshape(owners, per, terms + 2), "trade", 0, 0, tiled=False)
    got = got.reshape(count, terms + 2)
    got_coeffs = got[:, :terms].astype(jnp.bfloat16)
    got_col = got[:, terms].astype(jnp.int32)
    got_ns = got[:, terms + 1].astype(jnp.int32)

    moved = jnp.dot(
        drivers,
        lax.all_gather(loadings, "path", axis=0, tiled=True),
        preferred_element_type=jnp.float32,
    )
    factors = (start_state.astype(jnp.float32) + moved).astype(jnp.bfloat16)
    pick = (jnp.arange(width, dtype=jnp.int32)[:, None] == got_col[None, :]).astype(jnp.bfloat16)
    chosen = jnp.dot(factors, pick, preferred_element_type=jnp.float32).astype(jnp.bfloat16)
    values = clenshaw(chosen, got_coeffs.astype(jnp.float32).T)

    total_sets = ns_cp.shape[0] * owners
    net_table = (got_ns[:, None] == jnp.arange(total_sets, dtype=jnp.int32)[None, :]).astype(
        jnp.bfloat16
    )
    netting = jnp.dot(values, net_table, preferred_element_type=jnp.float32)
    shares = lax.psum_scatter(netting, "trade", scatter_dimension=1, tiled=True)
    positive = jnp.maximum(shares, 0.0).astype(jnp.bfloat16)
    cp_table = (ns_cp[:, None] == jnp.arange(CP_DEV * owners, dtype=jnp.int32)[None, :]).astype(
        jnp.bfloat16
    )
    partial_cp = jnp.dot(positive, cp_table, preferred_element_type=jnp.float32)
    exposure = lax.psum_scatter(partial_cp, "trade", scatter_dimension=1, tiled=True).T
    return exposure


def solution(mesh):
    return jax.shard_map(
        per_device,
        mesh=mesh,
        in_specs=(
            P("path", None),
            P("path", "trade"),
            P("path", "trade"),
            P("trade", None),
            P("trade"),
            P("trade"),
            P("trade"),
        ),
        out_specs=P("trade", "path"),
        check_vma=False,
    )
```

time: 522 us -> 328 us (0.63)
  other arithmetic: 119 us -> 3.07 us
  waiting for transfers between devices: 364 us -> 262 us
  blocking collectives: 0 us -> 33.1 us
  local copies, waits for them, and re-layouts: 13.8 us -> 0.47 us
    dot_general x8 -> x0, other arithmetic: 112 us -> none  [one_block(): jnp.einsum('ptk,tk->pt', basis, coeff_part.astype(jnp.float32), precision...]
    all_gather x1 -> x0, waiting for transfers between devices: 68.6 us -> none  [per_device(): whole = lax.all_gather(factors, 'trade', axis=1, tiled=True)]
    all_gather x1, waiting for transfers between devices: 172 us -> 135 us  [per_device(): lax.all_gather(loadings, 'path', axis=0, tiled=True)]
    all_to_all x0 -> x1, blocking collectives: none -> 33.1 us  [per_device(): lax.all_to_all(sent.reshape(owners, per, terms + 2), 'trade', 0, 0, tiled...]
    while x8 -> x0, other arithmetic: 6.11 us -> none
    dynamic_update_slice x16 -> x0, local copies, waits for them, and re-layouts: 5.82 us -> none  [valuation(): values = lax.map(one_block, (factor_blocks, coeff_blocks))]
    dot_general x1 -> x3, matrix products: 5.38 us -> 10.9 us  [the longest x1 8.68 us: per_device(): jnp.dot(factors, pick, preferred_element_type=jnp.float32)]
  transfers between devices with their start and end apart: 4 -> 3, of which waited for: 4 -> 3; matrix products, arithmetic and copies ran while one was open for 0% -> 2% of each run, Pallas kernels for 0% -> 0%
where the time goes in v1:
time: 328 us; the launch traced here: 327 us
  waiting for transfers between devices  262 us (80%)
  blocking collectives  33.1 us (10%)
  matrix products  15.6 us (5%)
  between operations  13.2 us (4%)
    all_gather x1, waiting for transfers between devices, per_device(): lax.all_gather(loadings, 'path', axis=0, tiled=True)  135 us
    reduce_scatter x1, waiting for transfers between devices, per_device(): shares = lax.psum_scatter(netting, 'trade', scatter_dimension=1, tiled=True)  67.2 us
    reduce_scatter x1, waiting for transfers between devices, per_device(): lax.psum_scatter(partial_cp, 'trade', scatter_dimension=1, tiled=True)  58.4 us
    all_to_all x1, blocking collectives, per_device(): lax.all_to_all(sent.reshape(owners, per, terms + 2), 'trade', 0, 0, tiled...  33.1 us
    dot_general x1, matrix products, per_device(): jnp.dot(factors, pick, preferred_element_type=jnp.float32)  8.68 us
  transfers between devices with their start and end apart: 3, of which 3 were waited for; matrix products, arithmetic and copies ran while one was open for 2% of the time, Pallas kernels for 0%

profile of v1, /device:TPU:6, one launch (start us, length us, event | category | flops | bytes accessed | tf_op | source)
XLA Modules:
  0.0 327.4 jit_solution(6888246618315880932)
XLA Ops:
  6.5 0.0 copy-start
  6.5 0.0 all-gather.2.cloned.1.call-start
  6.5 0.7 all-gather.2.cloned.1.call-update
  7.3 0.0 copy-start.2
  7.3 0.0 reduce-scatter.3.cloned.1.call-start
  7.3 1.0 convert_element_type.60
  8.3 0.7 convert_element_type.62
  9.0 0.7 add_select_fusion.1
  9.7 0.5 fusion.13
  10.1 0.7 fusion.39
  10.8 1.7 fusion.2
  12.6 0.1 copy.11
  12.7 0.1 copy.9
  12.7 33.1 %all_to_all.5 = f32[8,128,66]{1,2,0:T(8,128)S(1)} all-to-all(f32[8,128,66]{1,2,0:T(8,128)S(1)} %copy.9), channel_id=1, replica_groups=mesh['path'=64,'trade'=8] {'trade'}, dimensions={0} | all-to-all | bytes 540672 | tf_op jit(solution)/shard_map/all_to_all | solution.py:46
  45.8 0.1 copy.14
  45.9 0.1 copy.12
  46.1 0.1 fusion.46
  46.1 0.1 fusion.44
  46.2 0.1 fusion.45
  46.3 135.4 %all-gather.2.cloned.1.call-done = bf16[4096,1024]{1,0:T(8,128)(2,1)} async-done(((bf16[64,1024]{1,0:T(8,128)(2,1)}), bf16[4096,1024]{1,0:T(8,128)(2,1)}) %all-gather.2.cloned.1.call-update) | async-done | bytes 8388624 | tf_op jit(solution)/shard_map/all_gather | solution.py:54
  181.7 0.0 copy-done
  181.7 0.0 copy-done.2
  181.7 8.7 %subtract_convert_fusion = bf16[128,1024]{1,0:T(8,128)(2,1)S(1)} fusion(s32[1024]{0:T(1024)S(1)} %bitcast.159, bf16[128,4096]{1,0:T(8,128)(2,1)S(1)} %copy-done, bf16[4096,1024]{1,0:T(8,128)(2,1)} %all-gather.2.cloned.1.call-done, bf16[128,1024]{1,0:T(8,128)(2,1)S(1)} %copy-done.2, f32[1024]{0:T(1024)S(1)} %bitcast.120, f32[1024]{0:T(1024)S(1)} %bitcast.121, ...), kind=kOutput, calls=%fused_computation.19 | convolution fusion | flops 1369178112 | bytes 10227712 | tf_op jit(solution)/shard_map/dot_general | solution.py:59
  190.4 0.0 copy-start.1
  190.4 2.9 fusion
  193.3 0.0 reduce-scatter.3.cloned.1.call-update
  193.3 0.0 reduce-scatter.5.cloned.1.call-start
  193.3 67.2 %reduce-scatter.3.cloned.1.call-done = f32[128,256]{1,0:T(8,128)} async-done(((f32[128,2048]{1,0:T(8,128)}), f32[128,256]{1,0:T(8,128)}) %reduce-scatter.3.cloned.1.call-update) | async-done | bytes 131088 | tf_op jit(solution)/shard_map/reduce_scatter | solution.py:67
  260.6 0.0 copy-done.1
  260.6 1.9 fusion.34
  262.4 0.0 reduce-scatter.5.cloned.1.call-update
  262.5 58.4 %reduce-scatter.5.cloned.1.call-done = f32[128,32]{0,1:T(8,128)} async-done(((f32[128,256]{0,1:T(8,128)}), f32[128,32]{0,1:T(8,128)}) %reduce-scatter.5.cloned.1.call-update) | async-done | bytes 16400 | tf_op jit(solution)/shard_map/reduce_scatter | solution.py:73
  (5 shorter events, 0.1 us)
Async XLA Ops:
  6.5 175.1 %copy-start = (bf16[128,4096]{1,0:T(8,128)(2,1)S(1)}, bf16[128,4096]{1,0:T(8,128)(2,1)}, u32[]{:S(2)}) copy-start(bf16[128,4096]{1,0:T(8,128)(2,1)} %param.7) | copy-start | bytes 3145732
  6.5 175.1 %all-gather.2.cloned.1.call-start = ((), (), s32[]{:S(2)}) async-start(), calls=%async_computation.3 | async-start | bytes 8519680 | tf_op jit(solution)/shard_map/all_gather | solution.py:54
  7.3 174.4 %copy-start.2 = (bf16[128,1024]{1,0:T(8,128)(2,1)S(1)}, bf16[128,1024]{1,0:T(8,128)(2,1)}, u32[]{:S(2)}) copy-start(bf16[128,1024]{1,0:T(8,128)(2,1)} %param.9) | copy-start | bytes 786436
  7.3 253.3 %reduce-scatter.3.cloned.1.call-start = ((), (), s32[]{:S(2)}) async-start(), calls=%async_computation.4 | async-start | bytes 1179648 | tf_op jit(solution)/shard_map/reduce_scatter | solution.py:67
  190.4 70.2 %copy-start.1 = (s32[256]{0:T(256)S(1)}, s32[256]{0:T(256)}, u32[]{:S(2)}) copy-start(s32[256]{0:T(256)} %param.13) | copy-start | bytes 3076
  193.3 127.5 %reduce-scatter.5.cloned.1.call-start = ((), (), s32[]{:S(2)}) async-start(), calls=%async_computation.5 | async-start | bytes 147456 | tf_op jit(solution)/shard_map/reduce_scatter | solution.py:73
Sparse Core Ops, SparseCore 0:
  11.8 169.8 all-gather.1
  193.4 67.1 reduce-scatter.2
  263.3 57.4 reduce-scatter.4

commit v2 on v1

--- a/solution.py
+++ b/solution.py
@@ -1,7 +1,7 @@
 import jax
 import jax.numpy as jnp
 from jax import lax
-from jax.sharding import PartitionSpec as P
+from jax.sharding import Mesh, PartitionSpec as P
 
 CP_DEV = 32
 
@@ -49,11 +49,13 @@
     got_col = got[:, terms].astype(jnp.int32)
     got_ns = got[:, terms + 1].astype(jnp.int32)
 
-    moved = jnp.dot(
-        drivers,
-        lax.all_gather(loadings, "path", axis=0, tiled=True),
-        preferred_element_type=jnp.float32,
-    )
+    gathered = lax.all_gather(loadings, "zh", axis=0, tiled=True)
+    gathered = lax.all_gather(gathered, ("x", "y", "c"), axis=0, tiled=True)
+    rows = drivers.shape[0]
+    lead = loadings.shape[0]
+    sizes = [lax.axis_size(name) for name in PATH]
+    order = drivers.reshape(rows, *sizes, lead).transpose(0, 1, 3, 4, 2, 5).reshape(rows, -1)
+    moved = jnp.dot(order, gathered, preferred_element_type=jnp.float32)
     factors = (start_state.astype(jnp.float32) + moved).astype(jnp.bfloat16)
     pick = (jnp.arange(width, dtype=jnp.int32)[:, None] == got_col[None, :]).astype(jnp.bfloat16)
     chosen = jnp.dot(factors, pick, preferred_element_type=jnp.float32).astype(jnp.bfloat16)
@@ -70,23 +72,27 @@
         jnp.bfloat16
     )
     partial_cp = jnp.dot(positive, cp_table, preferred_element_type=jnp.float32)
-    exposure = lax.psum_scatter(partial_cp, "trade", scatter_dimension=1, tiled=True).T
-    return exposure
+    pieces = lax.all_to_all(partial_cp.reshape(rows, owners, CP_DEV), "trade", 1, 1, tiled=False)
+    return jnp.sum(pieces, axis=1).T
+
+
+PATH = ("x", "zh", "y", "c")
 
 
 def solution(mesh):
+    fine = Mesh(mesh.devices.reshape(4, 2, 4, 2, -1), PATH + ("trade",))
     return jax.shard_map(
         per_device,
-        mesh=mesh,
+        mesh=fine,
         in_specs=(
-            P("path", None),
-            P("path", "trade"),
-            P("path", "trade"),
+            P(PATH, None),
+            P(PATH, "trade"),
+            P(PATH, "trade"),
             P("trade", None),
             P("trade"),
             P("trade"),
             P("trade"),
         ),
-        out_specs=P("trade", "path"),
+        out_specs=P("trade", PATH),
         check_vma=False,
     )

time: 328 us -> 204 us (0.62)
  waiting for transfers between devices: 262 us -> 122 us
  starting transfers between devices: 0.08 us -> 13.6 us
    all_gather x1, waiting for transfers between devices: 135 us -> 36.7 us  [per_device(): gathered = lax.all_gather(gathered, ('x', 'y', 'c'), axis=0, tiled=True)]
    reduce_scatter x1 -> x0, waiting for transfers between devices: 58.4 us -> none  [per_device(): lax.psum_scatter(partial_cp, 'trade', scatter_dimension=1, tiled=True)]
    all_gather x0 -> x1, blocking collectives: none -> 20.2 us  [per_device(): gathered = lax.all_gather(loadings, 'zh', axis=0, tiled=True)]
    all_to_all x1, blocking collectives: 33.1 us -> 13.8 us  [per_device(): lax.all_to_all(partial_cp.reshape(rows, owners, CP_DEV), 'trade', 1, 1, t...]
    all_to_all x0 -> x1, waiting for transfers between devices: none -> 17.1 us  [per_device(): lax.all_to_all(sent.reshape(owners, per, terms + 2), 'trade', 0, 0, tiled...]
    all_to_all x0 -> x1, starting transfers between devices: none -> 13.6 us  [per_device(): lax.all_to_all(sent.reshape(owners, per, terms + 2), 'trade', 0, 0, tiled...]
  transfers between devices with their start and end apart: 3 -> 3, of which waited for: 3 -> 3; matrix products, arithmetic and copies ran while one was open for 2% -> 4% of each run, Pallas kernels for 0% -> 0%
where the time goes in v2:
time: 204 us
  waiting for transfers between devices  122 us (60%)
  blocking collectives  34.1 us (17%)
  matrix products  15 us (7%)
  starting transfers between devices  13.6 us (7%)
  between operations  13.6 us (7%)
  other arithmetic  3.66 us (2%)
    reduce_scatter x1, waiting for transfers between devices, per_device(): shares = lax.psum_scatter(netting, 'trade', scatter_dimension=1, tiled=True)  68 us
    all_gather x1, waiting for transfers between devices, per_device(): gathered = lax.all_gather(gathered, ('x', 'y', 'c'), axis=0, tiled=True)  36.7 us
    all_gather x1, blocking collectives, per_device(): gathered = lax.all_gather(loadings, 'zh', axis=0, tiled=True)  20.2 us
    all_to_all x1, waiting for transfers between devices, per_device(): lax.all_to_all(sent.reshape(owners, per, terms + 2), 'trade', 0, 0, tiled...  17.1 us
    all_to_all x1, blocking collectives, per_device(): lax.all_to_all(partial_cp.reshape(rows, owners, CP_DEV), 'trade', 1, 1, t...  13.8 us
    all_to_all x1, starting transfers between devices, per_device(): lax.all_to_all(sent.reshape(owners, per, terms + 2), 'trade', 0, 0, tiled...  13.6 us
    dot_general x1, matrix products, per_device(): jnp.dot(factors, pick, preferred_element_type=jnp.float32)  8.71 us
  transfers between devices with their start and end apart: 3, of which 3 were waited for; matrix products, arithmetic and copies ran while one was open for 4% of the time, Pallas kernels for 0%

profile of v2, /device:TPU:6, one launch (start us, length us, event | category | flops | bytes accessed | tf_op | source)
XLA Modules:
  0.0 203.7 jit_solution(4923286642422749071)
XLA Ops:
  6.5 0.0 copy-start
  6.5 0.0 all-gather.2.cloned.1.call-start
  6.5 20.2 %all_gather.6 = bf16[128,1024]{1,0:T(8,128)(2,1)} all-gather(bf16[64,1024]{1,0:T(8,128)(2,1)} %param.8), channel_id=1, replica_groups=mesh['x'=4,'zh'=2,'y'=4,'c'=2,'trade'=8] {'zh'}, dimensions={0}, use_global_device_ids=true | all-gather | bytes 393216 | tf_op jit(solution)/shard_map/all_gather | solution.py:52
  26.8 0.0 all-gather.2.cloned.1.call-update
  26.8 0.9 convert_element_type.60
  27.7 0.7 convert_element_type.62
  28.4 0.7 add_select_fusion.1
  29.1 0.5 fusion.13
  29.6 0.7 fusion.39
  30.3 1.7 fusion.2
  32.0 0.1 copy.21
  32.1 0.0 copy-start.2
  32.2 0.8 copy.15
  33.0 13.6 %all-to-all-start = ((f32[8,128,66]{1,2,0:T(8,128)}), f32[8,128,66]{1,2,0:T(8,128)S(1)}, u32[]{:S(2)}, u32[]{:S(2)}) async-start(f32[8,128,66]{1,2,0:T(8,128)} %copy.15), calls=%async_computation | async-start | bytes 589824 | tf_op jit(solution)/shard_map/all_to_all | solution.py:46
  46.5 0.0 reduce-scatter.2.cloned.1.call-start
  46.6 0.0 copy-done
  46.6 0.7 copy.17
  47.3 0.1 copy.18
  47.4 17.1 %all-to-all-done = f32[8,128,66]{1,2,0:T(8,128)S(1)} async-done(((f32[8,128,66]{1,2,0:T(8,128)}), f32[8,128,66]{1,2,0:T(8,128)S(1)}, u32[]{:S(2)}, u32[]{:S(2)}) %all-to-all-start) | async-done | bytes 270368 | tf_op jit(solution)/shard_map/all_to_all | solution.py:46
  64.4 0.1 copy.24
  64.5 0.1 copy.22
  64.7 0.1 fusion.46
  64.7 0.1 fusion.44
  64.8 0.1 fusion.45
  64.9 36.7 %all-gather.2.cloned.1.call-done = bf16[4096,1024]{1,0:T(8,128)(2,1)} async-done(((bf16[128,1024]{1,0:T(8,128)(2,1)}), bf16[4096,1024]{1,0:T(8,128)(2,1)}) %all-gather.2.cloned.1.call-update) | async-done | bytes 8388624 | tf_op jit(solution)/shard_map/all_gather | solution.py:53
  101.6 0.0 copy-done.2
  101.6 8.7 %subtract_convert_fusion = bf16[128,1024]{1,0:T(8,128)(2,1)S(1)} fusion(s32[1024]{0:T(1024)S(1)} %bitcast.167, bf16[128,4096]{0,1:T(8,128)(2,1)S(1)} %bitcast.96, bf16[4096,1024]{1,0:T(8,128)(2,1)} %all-gather.2.cloned.1.call-done, bf16[128,1024]{1,0:T(8,128)(2,1)S(1)} %copy-done.2, f32[1024]{0:T(1024)S(1)} %bitcast.128, f32[1024]{0:T(1024)S(1)} %bitcast.129, ...), kind=kOutput, calls=%fused_computation.19 | convolution fusion | flops 1369178112 | bytes 10227712 | tf_op jit(solution)/shard_map/dot_general | solution.py:61
  110.3 0.0 copy-start.1
  110.3 2.9 %fusion = f32[128,2048]{1,0:T(8,128)} fusion(bf16[128,1024]{1,0:T(8,128)(2,1)S(1)} %subtract_convert_fusion, s32[1024]{0:T(1024)S(1)} %bitcast.166), kind=kOutput, calls=%fused_computation.1 | convolution fusion | flops 538968064 | bytes 1314816 | tf_op jit(solution)/shard_map/dot_general | solution.py:68
  113.2 0.0 reduce-scatter.2.cloned.1.call-update
  113.2 68.0 %reduce-scatter.2.cloned.1.call-done = f32[128,256]{1,0:T(8,128)} async-done(((f32[128,2048]{1,0:T(8,128)}), f32[128,256]{1,0:T(8,128)}) %reduce-scatter.2.cloned.1.call-update) | async-done | bytes 131088 | tf_op jit(solution)/shard_map/reduce_scatter | solution.py:69
  181.2 0.0 copy-done.1
  181.2 1.2 fusion.34
  182.5 13.8 %all_to_all.10 = f32[128,8,32]{0,2,1:T(8,128)S(1)} all-to-all(f32[128,8,32]{0,2,1:T(8,128)S(1)} %bitcast.99), channel_id=1, replica_groups=mesh['x'=4,'zh'=2,'y'=4,'c'=2,'trade'=8] {'trade'}, dimensions={1} | all-to-all | bytes 262144 | tf_op jit(solution)/shard_map/all_to_all | solution.py:75
  196.3 0.6 reduce_sum.19
  (5 shorter events, 0.1 us)
Async XLA Ops:
  6.5 40.0 %copy-start = (bf16[128,4096]{1,0:T(8,128)(2,1)S(1)}, bf16[128,4096]{1,0:T(8,128)(2,1)}, u32[]{:S(2)}) copy-start(bf16[128,4096]{1,0:T(8,128)(2,1)} %param.7) | copy-start | bytes 3145732
  6.5 95.0 %all-gather.2.cloned.1.call-start = ((), (), s32[]{:S(2)}) async-start(), calls=%async_computation.3 | async-start | bytes 8650752 | tf_op jit(solution)/shard_map/all_gather | solution.py:53
  32.1 69.4 %copy-start.2 = (bf16[128,1024]{1,0:T(8,128)(2,1)S(1)}, bf16[128,1024]{1,0:T(8,128)(2,1)}, u32[]{:S(2)}) copy-start(bf16[128,1024]{1,0:T(8,128)(2,1)} %param.9) | copy-start | bytes 786436
  33.0 31.5 %all-to-all-start = ((f32[8,128,66]{1,2,0:T(8,128)}), f32[8,128,66]{1,2,0:T(8,128)S(1)}, u32[]{:S(2)}, u32[]{:S(2)}) async-start(f32[8,128,66]{1,2,0:T(8,128)} %copy.15), calls=%async_computation | async-start | bytes 589824 | tf_op jit(solution)/shard_map/all_to_all | solution.py:46
  46.5 134.7 %reduce-scatter.2.cloned.1.call-start = ((), (), s32[]{:S(2)}) async-start(), calls=%async_computation.4 | async-start | bytes 1179648 | tf_op jit(solution)/shard_map/reduce_scatter | solution.py:69
  110.3 70.9 %copy-start.1 = (s32[256]{0:T(256)S(1)}, s32[256]{0:T(256)}, u32[]{:S(2)}) copy-start(s32[256]{0:T(256)} %param.13) | copy-start | bytes 3076
Sparse Core Ops, SparseCore 0:
  26.9 74.5 all-gather.1
  113.3 67.8 reduce-scatter.1

commit v3 on v2

--- a/solution.py
+++ b/solution.py
@@ -29,6 +29,23 @@
     rank = jnp.sum(running * onehot.astype(jnp.float32), axis=1).astype(jnp.int32) - 1
     slot = block * per + rank
     return (slot[:, None] == jnp.arange(count, dtype=jnp.int32)[None, :]).astype(jnp.float32)
+
+
+def ring_reduce(parts, owners):
+    ring = list(range(0, owners, 2)) + list(range(owners - 1, 0, -2))
+    where = [ring.index(t) for t in range(owners)]
+    perm = [(ring[k], ring[(k + 1) % owners]) for k in range(owners)]
+    here = jnp.asarray(where, jnp.int32)[lax.axis_index("trade")]
+    ring_at = jnp.asarray(ring, jnp.int32)
+
+    def own(step):
+        owner = ring_at[(here - 1 - step) % owners]
+        return lax.dynamic_index_in_dim(parts, owner, axis=1, keepdims=False)
+
+    acc = own(0)
+    for step in range(1, owners):
+        acc = lax.ppermute(acc, "trade", perm) + own(step)
+    return acc
 
 
 def per_device(drivers, loadings, start_state, coeffs, trade_col, trade_ns, ns_cp):
@@ -66,7 +83,7 @@
         jnp.bfloat16
     )
     netting = jnp.dot(values, net_table, preferred_element_type=jnp.float32)
-    shares = lax.psum_scatter(netting, "trade", scatter_dimension=1, tiled=True)
+    shares = ring_reduce(netting.reshape(rows, owners, -1), owners)
     positive = jnp.maximum(shares, 0.0).astype(jnp.bfloat16)
     cp_table = (ns_cp[:, None] == jnp.arange(CP_DEV * owners, dtype=jnp.int32)[None, :]).astype(
         jnp.bfloat16

time: 204 us -> 204 us (level)
  waiting for transfers between devices: 122 us -> 49.9 us
  starting transfers between devices: 13.6 us -> 56 us
  between operations: 13.6 us -> 34.4 us
  blocking collectives: 34.1 us -> 41.3 us
  local copies, waits for them, and re-layouts: 1.98 us -> 4.34 us
    reduce_scatter x1 -> x0, waiting for transfers between devices: 68 us -> none  [per_device(): shares = lax.psum_scatter(netting, 'trade', scatter_dimension=1, tiled=True)]
    ppermute x0 -> x7, starting transfers between devices: none -> 42.5 us  [ring_reduce(): acc = lax.ppermute(acc, 'trade', perm) + own(step)]
    ppermute x0 -> x7, waiting for transfers between devices: none -> 18.1 us  [ring_reduce(): acc = lax.ppermute(acc, 'trade', perm) + own(step)]
    all_to_all x1, waiting for transfers between devices: 17.1 us -> 0.01 us  [per_device(): lax.all_to_all(sent.reshape(owners, per, terms + 2), 'trade', 0, 0, tiled...]
    all_to_all x1, blocking collectives: 13.8 us -> 21 us  [per_device(): lax.all_to_all(partial_cp.reshape(rows, owners, CP_DEV), 'trade', 1, 1, t...]
    all_gather x1, waiting for transfers between devices: 36.7 us -> 31.8 us  [per_device(): gathered = lax.all_gather(gathered, ('x', 'y', 'c'), axis=0, tiled=True)]
  transfers between devices with their start and end apart: 3 -> 9, of which waited for: 3 -> 8; matrix products, arithmetic and copies ran while one was open for 4% -> 4% of each run, Pallas kernels for 0% -> 0%
where the time goes in v3:
time: 204 us; the launch traced here: 203 us
  starting transfers between devices  56 us (27%)
  waiting for transfers between devices  49.9 us (24%)
  blocking collectives  41.3 us (20%)
  between operations  34.4 us (17%)
  matrix products  13.1 us (6%)
  local copies, waits for them, and re-layouts  4.34 us (2%)
  other arithmetic  3.76 us (2%)
    ppermute x7, starting transfers between devices, ring_reduce(): acc = lax.ppermute(acc, 'trade', perm) + own(step)  42.5 us
    all_gather x1, waiting for transfers between devices, per_device(): gathered = lax.all_gather(gathered, ('x', 'y', 'c'), axis=0, tiled=True)  31.8 us
    all_to_all x1, blocking collectives, per_device(): lax.all_to_all(partial_cp.reshape(rows, owners, CP_DEV), 'trade', 1, 1, t...  21 us
    all_gather x1, blocking collectives, per_device(): gathered = lax.all_gather(loadings, 'zh', axis=0, tiled=True)  20.3 us
    ppermute x7, waiting for transfers between devices, ring_reduce(): acc = lax.ppermute(acc, 'trade', perm) + own(step)  18.1 us
    all_to_all x1, starting transfers between devices, per_device(): lax.all_to_all(sent.reshape(owners, per, terms + 2), 'trade', 0, 0, tiled...  13.6 us
    dot_general x1, matrix products, per_device(): jnp.dot(factors, pick, preferred_element_type=jnp.float32)  8.7 us
  transfers between devices with their start and end apart: 9, of which 8 were waited for; matrix products, arithmetic and copies ran while one was open for 4% of the time, Pallas kernels for 0%

profile of v3, /device:TPU:6, one launch (start us, length us, event | category | flops | bytes accessed | tf_op | source)
XLA Modules:
  0.0 202.9 jit_solution(15636417659719394723)
XLA Ops:
  6.5 0.0 copy-start.4
  6.5 0.0 copy-start.1
  6.5 0.0 copy-start
  6.5 0.0 all-gather.2.cloned.1.call-start
  6.5 20.3 %all_gather.6 = bf16[128,1024]{1,0:T(8,128)(2,1)} all-gather(bf16[64,1024]{1,0:T(8,128)(2,1)} %param.10), channel_id=1, replica_groups=mesh['x'=4,'zh'=2,'y'=4,'c'=2,'trade'=8] {'zh'}, dimensions={0}, use_global_device_ids=true | all-gather | bytes 393216 | tf_op jit(solution)/shard_map/all_gather | solution.py:69
  26.8 0.0 all-gather.2.cloned.1.call-update
  26.8 0.9 convert_element_type.60
  27.8 0.7 convert_element_type.62
  28.5 0.7 add_select_fusion.1
  29.1 0.5 fusion.13
  29.6 0.7 fusion.42
  30.3 1.7 fusion.2
  32.1 0.1 copy.31
  32.2 0.0 copy-start.3
  32.2 0.8 copy.17
  33.0 13.6 %all-to-all-start = ((f32[8,128,66]{1,2,0:T(8,128)}), f32[8,128,66]{1,2,0:T(8,128)S(1)}, u32[]{:S(2)}, u32[]{:S(2)}) async-start(f32[8,128,66]{1,2,0:T(8,128)} %copy.17), calls=%async_computation | async-start | bytes 589824 | tf_op jit(solution)/shard_map/all_to_all | solution.py:63
  46.5 0.0 copy-done.4
  46.5 0.6 dynamic_slice.52
  52.5 0.0 copy-done.1
  52.5 0.7 fusion.51
  63.4 0.0 copy-done
  63.4 0.7 copy.19
  64.1 0.1 copy.20
  69.4 0.0 all-to-all-done
  69.4 0.1 copy.44
  69.5 0.1 copy.32
  69.6 0.1 fusion.49
  69.7 0.1 fusion.47
  69.7 0.1 fusion.48
  69.8 31.8 %all-gather.2.cloned.1.call-done = bf16[4096,1024]{1,0:T(8,128)(2,1)} async-done(((bf16[128,1024]{1,0:T(8,128)(2,1)}), bf16[4096,1024]{1,0:T(8,128)(2,1)}) %all-gather.2.cloned.1.call-update) | async-done | bytes 8388624 | tf_op jit(solution)/shard_map/all_gather | solution.py:70
  101.6 0.0 copy-done.3
  101.6 8.7 %subtract_convert_fusion = bf16[128,1024]{1,0:T(8,128)(2,1)S(1)} fusion(s32[1024]{0:T(1024)S(1)} %bitcast.210, bf16[128,4096]{0,1:T(8,128)(2,1)S(1)} %bitcast.137, bf16[4096,1024]{1,0:T(8,128)(2,1)} %all-gather.2.cloned.1.call-done, bf16[128,1024]{1,0:T(8,128)(2,1)S(1)} %copy-done.3, f32[1024]{0:T(1024)S(1)} %bitcast.171, f32[1024]{0:T(1024)S(1)} %bitcast.172, ...), kind=kOutput, calls=%fused_computation.19 | convolution fusion | flops 1369178112 | bytes 10227712 | tf_op jit(solution)/shard_map/dot_general | solution.py:78
  110.3 1.9 fusion
  112.2 0.0 copy-start.2
  112.2 0.3 copy.33
  112.5 0.7 constant_dynamic-slice_fusion
  113.3 4.5 %collective-permute-start = (f32[128,256]{1,0:T(8,128)S(1)}, f32[128,256]{1,0:T(8,128)S(1)}, u32[]{:S(2)}, u32[]{:S(2)}) collective-permute-start(f32[128,256]{1,0:T(8,128)S(1)} %bitcast.143), channel_id=1, source_target_pairs={{0,2},{2,4},{4,6},{6,7},{7,5},{5,3},{3,1},{1,0},{8,10},{10,12},{12... | collective-permute-start | bytes 393224 | tf_op jit(solution)/shard_map/ppermute | solution.py:47
  117.8 3.1 %collective-permute-done = f32[128,256]{1,0:T(8,128)S(1)} collective-permute-done((f32[128,256]{1,0:T(8,128)S(1)}, f32[128,256]{1,0:T(8,128)S(1)}, u32[]{:S(2)}, u32[]{:S(2)}) %collective-permute-start) | collective-permute-done | bytes 131104 | tf_op jit(solution)/shard_map/ppermute | solution.py:47
  120.9 5.7 %collective-permute-start.1 = (f32[128,256]{1,0:T(8,128)S(1)}, f32[128,256]{1,0:T(8,128)S(1)}, u32[]{:S(2)}, u32[]{:S(2)}) collective-permute-start(f32[128,256]{1,0:T(8,128)S(1)} %bitcast_add_fusion.6), channel_id=1, source_target_pairs={{0,2},{2,4},{4,6},{6,7},{7,5},{5,3},{3,1},{1,0},{8,10},{10,12},{12... | collective-permute-start | bytes 393224 | tf_op jit(solution)/shard_map/ppermute | solution.py:47
  126.6 2.5 %collective-permute-done.1 = f32[128,256]{1,0:T(8,128)S(1)} collective-permute-done((f32[128,256]{1,0:T(8,128)S(1)}, f32[128,256]{1,0:T(8,128)S(1)}, u32[]{:S(2)}, u32[]{:S(2)}) %collective-permute-start.1) | collective-permute-done | bytes 131104 | tf_op jit(solution)/shard_map/ppermute | solution.py:47
  129.1 6.5 %collective-permute-start.2 = (f32[128,256]{1,0:T(8,128)S(1)}, f32[128,256]{1,0:T(8,128)S(1)}, u32[]{:S(2)}, u32[]{:S(2)}) collective-permute-start(f32[128,256]{1,0:T(8,128)S(1)} %bitcast_add_fusion.5), channel_id=1, source_target_pairs={{0,2},{2,4},{4,6},{6,7},{7,5},{5,3},{3,1},{1,0},{8,10},{10,12},{12... | collective-permute-start | bytes 393224 | tf_op jit(solution)/shard_map/ppermute | solution.py:47
  135.6 2.5 %collective-permute-done.2 = f32[128,256]{1,0:T(8,128)S(1)} collective-permute-done((f32[128,256]{1,0:T(8,128)S(1)}, f32[128,256]{1,0:T(8,128)S(1)}, u32[]{:S(2)}, u32[]{:S(2)}) %collective-permute-start.2) | collective-permute-done | bytes 131104 | tf_op jit(solution)/shard_map/ppermute | solution.py:47
  138.2 6.5 %collective-permute-start.3 = (f32[128,256]{1,0:T(8,128)S(1)}, f32[128,256]{1,0:T(8,128)S(1)}, u32[]{:S(2)}, u32[]{:S(2)}) collective-permute-start(f32[128,256]{1,0:T(8,128)S(1)} %bitcast_add_fusion.4), channel_id=1, source_target_pairs={{0,2},{2,4},{4,6},{6,7},{7,5},{5,3},{3,1},{1,0},{8,10},{10,12},{12... | collective-permute-start | bytes 393224 | tf_op jit(solution)/shard_map/ppermute | solution.py:47
  144.6 2.5 %collective-permute-done.3 = f32[128,256]{1,0:T(8,128)S(1)} collective-permute-done((f32[128,256]{1,0:T(8,128)S(1)}, f32[128,256]{1,0:T(8,128)S(1)}, u32[]{:S(2)}, u32[]{:S(2)}) %collective-permute-start.3) | collective-permute-done | bytes 131104 | tf_op jit(solution)/shard_map/ppermute | solution.py:47
  147.2 6.5 %collective-permute-start.4 = (f32[128,256]{1,0:T(8,128)S(1)}, f32[128,256]{1,0:T(8,128)S(1)}, u32[]{:S(2)}, u32[]{:S(2)}) collective-permute-start(f32[128,256]{1,0:T(8,128)S(1)} %bitcast_add_fusion.3), channel_id=1, source_target_pairs={{0,2},{2,4},{4,6},{6,7},{7,5},{5,3},{3,1},{1,0},{8,10},{10,12},{12... | collective-permute-start | bytes 393224 | tf_op jit(solution)/shard_map/ppermute | solution.py:47
  153.6 2.5 %collective-permute-done.4 = f32[128,256]{1,0:T(8,128)S(1)} collective-permute-done((f32[128,256]{1,0:T(8,128)S(1)}, f32[128,256]{1,0:T(8,128)S(1)}, u32[]{:S(2)}, u32[]{:S(2)}) %collective-permute-start.4) | collective-permute-done | bytes 131104 | tf_op jit(solution)/shard_map/ppermute | solution.py:47
  156.1 6.5 %collective-permute-start.5 = (f32[128,256]{1,0:T(8,128)S(1)}, f32[128,256]{1,0:T(8,128)S(1)}, u32[]{:S(2)}, u32[]{:S(2)}) collective-permute-start(f32[128,256]{1,0:T(8,128)S(1)} %bitcast_add_fusion.2), channel_id=1, source_target_pairs={{0,2},{2,4},{4,6},{6,7},{7,5},{5,3},{3,1},{1,0},{8,10},{10,12},{12... | collective-permute-start | bytes 393224 | tf_op jit(solution)/shard_map/ppermute | solution.py:47
  162.6 2.5 %collective-permute-done.5 = f32[128,256]{1,0:T(8,128)S(1)} collective-permute-done((f32[128,256]{1,0:T(8,128)S(1)}, f32[128,256]{1,0:T(8,128)S(1)}, u32[]{:S(2)}, u32[]{:S(2)}) %collective-permute-start.5) | collective-permute-done | bytes 131104 | tf_op jit(solution)/shard_map/ppermute | solution.py:47
  165.1 6.5 %collective-permute-start.6 = (f32[128,256]{1,0:T(8,128)S(1)}, f32[128,256]{1,0:T(8,128)S(1)}, u32[]{:S(2)}, u32[]{:S(2)}) collective-permute-start(f32[128,256]{1,0:T(8,128)S(1)} %bitcast_add_fusion.1), channel_id=1, source_target_pairs={{0,2},{2,4},{4,6},{6,7},{7,5},{5,3},{3,1},{1,0},{8,10},{10,12},{12... | collective-permute-start | bytes 393224 | tf_op jit(solution)/shard_map/ppermute | solution.py:47
  171.6 2.5 %collective-permute-done.6 = f32[128,256]{1,0:T(8,128)S(1)} collective-permute-done((f32[128,256]{1,0:T(8,128)S(1)}, f32[128,256]{1,0:T(8,128)S(1)}, u32[]{:S(2)}, u32[]{:S(2)}) %collective-permute-start.6) | collective-permute-done | bytes 131104 | tf_op jit(solution)/shard_map/ppermute | solution.py:47
  174.1 0.0 copy-done.2
  174.1 0.3 fusion.34
  174.4 21.0 %all_to_all.10 = f32[128,8,32]{0,2,1:T(8,128)S(1)} all-to-all(f32[128,8,32]{0,2,1:T(8,128)S(1)} %bitcast.141), channel_id=1, replica_groups=mesh['x'=4,'zh'=2,'y'=4,'c'=2,'trade'=8] {'trade'}, dimensions={1} | all-to-all | bytes 262144 | tf_op jit(solution)/shard_map/all_to_all | solution.py:92
  195.5 0.6 reduce_sum.19
  (12 shorter events, 0.2 us)
Async XLA Ops:
  6.5 40.0 %copy-start.4 = (s32[8]{0:T(128)S(1)}, s32[8]{0:T(128)}, u32[]{:S(2)}) copy-start(s32[8]{0:T(128)} %constant.143.clone) | copy-start | bytes 100
  6.5 45.9 %copy-start.1 = (s32[8]{0:T(128)S(1)}, s32[8]{0:T(128)}, u32[]{:S(2)}) copy-start(s32[8]{0:T(128)} %constant.144.clone) | copy-start | bytes 100
  6.5 56.9 %copy-start = (bf16[128,4096]{1,0:T(8,128)(2,1)S(1)}, bf16[128,4096]{1,0:T(8,128)(2,1)}, u32[]{:S(2)}) copy-start(bf16[128,4096]{1,0:T(8,128)(2,1)} %param.9) | copy-start | bytes 3145732
  6.5 95.0 %all-gather.2.cloned.1.call-start = ((), (), s32[]{:S(2)}) async-start(), calls=%async_computation.2 | async-start | bytes 8650752 | tf_op jit(solution)/shard_map/all_gather | solution.py:70
  32.2 69.4 %copy-start.3 = (bf16[128,1024]{1,0:T(8,128)(2,1)S(1)}, bf16[128,1024]{1,0:T(8,128)(2,1)}, u32[]{:S(2)}) copy-start(bf16[128,1024]{1,0:T(8,128)(2,1)} %param.11) | copy-start | bytes 786436
  33.0 36.4 %all-to-all-start = ((f32[8,128,66]{1,2,0:T(8,128)}), f32[8,128,66]{1,2,0:T(8,128)S(1)}, u32[]{:S(2)}, u32[]{:S(2)}) async-start(f32[8,128,66]{1,2,0:T(8,128)} %copy.17), calls=%async_computation | async-start | bytes 589824 | tf_op jit(solution)/shard_map/all_to_all | solution.py:63
  112.2 61.9 %copy-start.2 = (s32[256]{0:T(256)S(1)}, s32[256]{0:T(256)}, u32[]{:S(2)}) copy-start(s32[256]{0:T(256)} %param.15) | copy-start | bytes 3076
  113.3 7.6 %collective-permute-start = (f32[128,256]{1,0:T(8,128)S(1)}, f32[128,256]{1,0:T(8,128)S(1)}, u32[]{:S(2)}, u32[]{:S(2)}) collective-permute-start(f32[128,256]{1,0:T(8,128)S(1)} %bitcast.143), channel_id=1, source_target_pairs={{0,2},{2,4},{4,6},{6,7},{7,5},{5,3},{3,1},{1,0},{8,10},{10,12},{12... | collective-permute-start | bytes 393224 | tf_op jit(solution)/shard_map/ppermute | solution.py:47
  120.9 8.2 %collective-permute-start.1 = (f32[128,256]{1,0:T(8,128)S(1)}, f32[128,256]{1,0:T(8,128)S(1)}, u32[]{:S(2)}, u32[]{:S(2)}) collective-permute-start(f32[128,256]{1,0:T(8,128)S(1)} %bitcast_add_fusion.6), channel_id=1, source_target_pairs={{0,2},{2,4},{4,6},{6,7},{7,5},{5,3},{3,1},{1,0},{8,10},{10,12},{12... | collective-permute-start | bytes 393224 | tf_op jit(solution)/shard_map/ppermute | solution.py:47
  129.1 9.0 %collective-permute-start.2 = (f32[128,256]{1,0:T(8,128)S(1)}, f32[128,256]{1,0:T(8,128)S(1)}, u32[]{:S(2)}, u32[]{:S(2)}) collective-permute-start(f32[128,256]{1,0:T(8,128)S(1)} %bitcast_add_fusion.5), channel_id=1, source_target_pairs={{0,2},{2,4},{4,6},{6,7},{7,5},{5,3},{3,1},{1,0},{8,10},{10,12},{12... | collective-permute-start | bytes 393224 | tf_op jit(solution)/shard_map/ppermute | solution.py:47
  138.2 9.0 %collective-permute-start.3 = (f32[128,256]{1,0:T(8,128)S(1)}, f32[128,256]{1,0:T(8,128)S(1)}, u32[]{:S(2)}, u32[]{:S(2)}) collective-permute-start(f32[128,256]{1,0:T(8,128)S(1)} %bitcast_add_fusion.4), channel_id=1, source_target_pairs={{0,2},{2,4},{4,6},{6,7},{7,5},{5,3},{3,1},{1,0},{8,10},{10,12},{12... | collective-permute-start | bytes 393224 | tf_op jit(solution)/shard_map/ppermute | solution.py:47
  147.2 9.0 %collective-permute-start.4 = (f32[128,256]{1,0:T(8,128)S(1)}, f32[128,256]{1,0:T(8,128)S(1)}, u32[]{:S(2)}, u32[]{:S(2)}) collective-permute-start(f32[128,256]{1,0:T(8,128)S(1)} %bitcast_add_fusion.3), channel_id=1, source_target_pairs={{0,2},{2,4},{4,6},{6,7},{7,5},{5,3},{3,1},{1,0},{8,10},{10,12},{12... | collective-permute-start | bytes 393224 | tf_op jit(solution)/shard_map/ppermute | solution.py:47
  156.1 9.0 %collective-permute-start.5 = (f32[128,256]{1,0:T(8,128)S(1)}, f32[128,256]{1,0:T(8,128)S(1)}, u32[]{:S(2)}, u32[]{:S(2)}) collective-permute-start(f32[128,256]{1,0:T(8,128)S(1)} %bitcast_add_fusion.2), channel_id=1, source_target_pairs={{0,2},{2,4},{4,6},{6,7},{7,5},{5,3},{3,1},{1,0},{8,10},{10,12},{12... | collective-permute-start | bytes 393224 | tf_op jit(solution)/shard_map/ppermute | solution.py:47
  165.1 9.0 %collective-permute-start.6 = (f32[128,256]{1,0:T(8,128)S(1)}, f32[128,256]{1,0:T(8,128)S(1)}, u32[]{:S(2)}, u32[]{:S(2)}) collective-permute-start(f32[128,256]{1,0:T(8,128)S(1)} %bitcast_add_fusion.1), channel_id=1, source_target_pairs={{0,2},{2,4},{4,6},{6,7},{7,5},{5,3},{3,1},{1,0},{8,10},{10,12},{12... | collective-permute-start | bytes 393224 | tf_op jit(solution)/shard_map/ppermute | solution.py:47
Sparse Core Ops, SparseCore 0:
  27.0 74.5 all-gather.1

commit v4 on v3

--- a/solution.py
+++ b/solution.py
@@ -83,7 +83,7 @@
         jnp.bfloat16
     )
     netting = jnp.dot(values, net_table, preferred_element_type=jnp.float32)
-    shares = ring_reduce(netting.reshape(rows, owners, -1), owners)
+    shares = jnp.sum(lax.all_to_all(netting.reshape(rows, owners, -1), "trade", 1, 1, tiled=False), axis=1)
     positive = jnp.maximum(shares, 0.0).astype(jnp.bfloat16)
     cp_table = (ns_cp[:, None] == jnp.arange(CP_DEV * owners, dtype=jnp.int32)[None, :]).astype(
         jnp.bfloat16

time: 204 us -> 198 us (0.971)
  blocking collectives: 41.3 us -> 97.2 us
  starting transfers between devices: 56 us -> 13.6 us
  between operations: 34.4 us -> 13.6 us
  waiting for transfers between devices: 49.9 us -> 53.9 us
  local copies, waits for them, and re-layouts: 4.34 us -> 2.06 us
    all_to_all x0 -> x1, blocking collectives: none -> 61.4 us  [per_device(): lax.all_to_all(netting.reshape(rows, owners, -1), 'trade', 1, 1, tiled=Fa...]
    ppermute x7 -> x0, starting transfers between devices: 42.5 us -> none  [ring_reduce(): acc = lax.ppermute(acc, 'trade', perm) + own(step)]
    ppermute x7 -> x0, waiting for transfers between devices: 18.1 us -> none  [ring_reduce(): acc = lax.ppermute(acc, 'trade', perm) + own(step)]
    all_to_all x1, waiting for transfers between devices: 0.01 us -> 17.1 us  [per_device(): lax.all_to_all(sent.reshape(owners, per, terms + 2), 'trade', 0, 0, tiled...]
    all_to_all x1, blocking collectives: 21 us -> 15.6 us  [per_device(): lax.all_to_all(partial_cp.reshape(rows, owners, CP_DEV), 'trade', 1, 1, t...]
    all_gather x1, waiting for transfers between devices: 31.8 us -> 36.7 us  [per_device(): gathered = lax.all_gather(gathered, ('x', 'y', 'c'), axis=0, tiled=True)]
  transfers between devices with their start and end apart: 9 -> 2, of which waited for: 8 -> 2; matrix products, arithmetic and copies ran while one was open for 4% -> 4% of each run, Pallas kernels for 0% -> 0%
where the time goes in v4:
time: 198 us; the launch traced here: 197 us
  blocking collectives  97.2 us (49%)
  waiting for transfers between devices  53.9 us (27%)
  starting transfers between devices  13.6 us (7%)
  between operations  13.6 us (7%)
  matrix products  13.1 us (7%)
  other arithmetic  3.73 us (2%)
  local copies, waits for them, and re-layouts  2.06 us (1%)
    all_to_all x1, blocking collectives, per_device(): lax.all_to_all(netting.reshape(rows, owners, -1), 'trade', 1, 1, tiled=Fa...  61.4 us
    all_gather x1, waiting for transfers between devices, per_device(): gathered = lax.all_gather(gathered, ('x', 'y', 'c'), axis=0, tiled=True)  36.7 us
    all_gather x1, blocking collectives, per_device(): gathered = lax.all_gather(loadings, 'zh', axis=0, tiled=True)  20.3 us
    all_to_all x1, waiting for transfers between devices, per_device(): lax.all_to_all(sent.reshape(owners, per, terms + 2), 'trade', 0, 0, tiled...  17.1 us
    all_to_all x1, blocking collectives, per_device(): lax.all_to_all(partial_cp.reshape(rows, owners, CP_DEV), 'trade', 1, 1, t...  15.6 us
    all_to_all x1, starting transfers between devices, per_device(): lax.all_to_all(sent.reshape(owners, per, terms + 2), 'trade', 0, 0, tiled...  13.6 us
    dot_general x1, matrix products, per_device(): jnp.dot(factors, pick, preferred_element_type=jnp.float32)  8.71 us
  transfers between devices with their start and end apart: 2, of which 2 were waited for; matrix products, arithmetic and copies ran while one was open for 4% of the time, Pallas kernels for 0%

profile of v4, /device:TPU:6, one launch (start us, length us, event | category | flops | bytes accessed | tf_op | source)
XLA Modules:
  0.0 197.1 jit_solution(9778004533216431658)
XLA Ops:
  6.5 0.0 copy-start
  6.5 0.0 all-gather.2.cloned.1.call-start
  6.5 20.3 %all_gather.6 = bf16[128,1024]{1,0:T(8,128)(2,1)} all-gather(bf16[64,1024]{1,0:T(8,128)(2,1)} %param.8), channel_id=1, replica_groups=mesh['x'=4,'zh'=2,'y'=4,'c'=2,'trade'=8] {'zh'}, dimensions={0}, use_global_device_ids=true | all-gather | bytes 393216 | tf_op jit(solution)/shard_map/all_gather | solution.py:69
  26.8 0.0 all-gather.2.cloned.1.call-update
  26.8 0.9 convert_element_type.60
  27.7 0.7 convert_element_type.62
  28.4 0.7 add_select_fusion.1
  29.1 0.5 fusion.13
  29.6 0.7 fusion.39
  30.3 1.7 fusion.2
  32.1 0.1 copy.24
  32.1 0.0 copy-start.2
  32.2 0.8 copy.16
  33.0 13.6 %all-to-all-start = ((f32[8,128,66]{1,2,0:T(8,128)}), f32[8,128,66]{1,2,0:T(8,128)S(1)}, u32[]{:S(2)}, u32[]{:S(2)}) async-start(f32[8,128,66]{1,2,0:T(8,128)} %copy.16), calls=%async_computation | async-start | bytes 589824 | tf_op jit(solution)/shard_map/all_to_all | solution.py:63
  46.5 0.0 copy-done
  46.5 0.7 copy.18
  47.2 0.1 copy.19
  47.3 17.1 %all-to-all-done = f32[8,128,66]{1,2,0:T(8,128)S(1)} async-done(((f32[8,128,66]{1,2,0:T(8,128)}), f32[8,128,66]{1,2,0:T(8,128)S(1)}, u32[]{:S(2)}, u32[]{:S(2)}) %all-to-all-start) | async-done | bytes 270368 | tf_op jit(solution)/shard_map/all_to_all | solution.py:63
  64.4 0.1 copy.29
  64.5 0.1 copy.25
  64.7 0.1 fusion.46
  64.7 0.1 fusion.44
  64.8 0.1 fusion.45
  64.9 36.7 %all-gather.2.cloned.1.call-done = bf16[4096,1024]{1,0:T(8,128)(2,1)} async-done(((bf16[128,1024]{1,0:T(8,128)(2,1)}), bf16[4096,1024]{1,0:T(8,128)(2,1)}) %all-gather.2.cloned.1.call-update) | async-done | bytes 8388624 | tf_op jit(solution)/shard_map/all_gather | solution.py:70
  101.6 0.0 copy-done.2
  101.6 8.7 %subtract_convert_fusion = bf16[128,1024]{1,0:T(8,128)(2,1)S(1)} fusion(s32[1024]{0:T(1024)S(1)} %bitcast.173, bf16[128,4096]{0,1:T(8,128)(2,1)S(1)} %bitcast.101, bf16[4096,1024]{1,0:T(8,128)(2,1)} %all-gather.2.cloned.1.call-done, bf16[128,1024]{1,0:T(8,128)(2,1)S(1)} %copy-done.2, f32[1024]{0:T(1024)S(1)} %bitcast.134, f32[1024]{0:T(1024)S(1)} %bitcast.135, ...), kind=kOutput, calls=%fused_computation.20 | convolution fusion | flops 1369178112 | bytes 10227712 | tf_op jit(solution)/shard_map/dot_general | solution.py:78
  110.3 0.0 copy-start.1
  110.3 1.9 fusion
  112.2 0.1 copy.28
  112.3 61.4 %all_to_all.15 = f32[128,8,256]{2,0,1:T(8,128)S(1)} all-to-all(f32[128,8,256]{2,0,1:T(8,128)S(1)} %bitcast.96), channel_id=1, replica_groups=mesh['x'=4,'zh'=2,'y'=4,'c'=2,'trade'=8] {'trade'}, dimensions={1} | all-to-all | bytes 2097152 | tf_op jit(solution)/shard_map/all_to_all | solution.py:86
  173.7 0.1 reduce_sum.28
  173.8 0.0 copy-done.1
  173.8 0.3 fusion.34
  174.1 15.6 %all_to_all.16 = f32[128,8,32]{0,2,1:T(8,128)S(1)} all-to-all(f32[128,8,32]{0,2,1:T(8,128)S(1)} %bitcast.105), channel_id=1, replica_groups=mesh['x'=4,'zh'=2,'y'=4,'c'=2,'trade'=8] {'trade'}, dimensions={1} | all-to-all | bytes 262144 | tf_op jit(solution)/shard_map/all_to_all | solution.py:92
  189.7 0.6 reduce_sum.29
  (5 shorter events, 0.1 us)
Async XLA Ops:
  6.5 40.0 %copy-start = (bf16[128,4096]{1,0:T(8,128)(2,1)S(1)}, bf16[128,4096]{1,0:T(8,128)(2,1)}, u32[]{:S(2)}) copy-start(bf16[128,4096]{1,0:T(8,128)(2,1)} %param.7) | copy-start | bytes 3145732
  6.5 95.0 %all-gather.2.cloned.1.call-start = ((), (), s32[]{:S(2)}) async-start(), calls=%async_computation.3 | async-start | bytes 8650752 | tf_op jit(solution)/shard_map/all_gather | solution.py:70
  32.1 69.4 %copy-start.2 = (bf16[128,1024]{1,0:T(8,128)(2,1)S(1)}, bf16[128,1024]{1,0:T(8,128)(2,1)}, u32[]{:S(2)}) copy-start(bf16[128,1024]{1,0:T(8,128)(2,1)} %param.9) | copy-start | bytes 786436
  33.0 31.5 %all-to-all-start = ((f32[8,128,66]{1,2,0:T(8,128)}), f32[8,128,66]{1,2,0:T(8,128)S(1)}, u32[]{:S(2)}, u32[]{:S(2)}) async-start(f32[8,128,66]{1,2,0:T(8,128)} %copy.16), calls=%async_computation | async-start | bytes 589824 | tf_op jit(solution)/shard_map/all_to_all | solution.py:63
  110.3 63.5 %copy-start.1 = (s32[256]{0:T(256)S(1)}, s32[256]{0:T(256)}, u32[]{:S(2)}) copy-start(s32[256]{0:T(256)} %param.13) | copy-start | bytes 3076
Sparse Core Ops, SparseCore 0:
  26.9 74.5 all-gather.1

commit v5 on v4

--- a/solution.py
+++ b/solution.py
@@ -83,7 +83,8 @@
         jnp.bfloat16
     )
     netting = jnp.dot(values, net_table, preferred_element_type=jnp.float32)
-    shares = jnp.sum(lax.all_to_all(netting.reshape(rows, owners, -1), "trade", 1, 1, tiled=False), axis=1)
+    sent = netting.astype(jnp.bfloat16).reshape(rows, owners, -1)
+    shares = jnp.sum(lax.all_to_all(sent, "trade", 1, 1, tiled=False).astype(jnp.float32), axis=1)
     positive = jnp.maximum(shares, 0.0).astype(jnp.bfloat16)
     cp_table = (ns_cp[:, None] == jnp.arange(CP_DEV * owners, dtype=jnp.int32)[None, :]).astype(
         jnp.bfloat16

time: 198 us -> 175 us (0.88)
  blocking collectives: 97.2 us -> 74.8 us
    all_to_all x1, blocking collectives: 61.4 us -> 38.9 us  [per_device(): lax.all_to_all(sent, 'trade', 1, 1, tiled=False).astype(jnp.float32)]
where the time goes in v5:
time: 175 us
  blocking collectives  74.8 us (43%)
  waiting for transfers between devices  53.9 us (31%)
  starting transfers between devices  13.6 us (8%)
  between operations  13.6 us (8%)
  matrix products  13.1 us (7%)
  other arithmetic  3.73 us (2%)
  local copies, waits for them, and re-layouts  2 us (1%)
    all_to_all x1, blocking collectives, per_device(): lax.all_to_all(sent, 'trade', 1, 1, tiled=False).astype(jnp.float32)  38.9 us
    all_gather x1, waiting for transfers between devices, per_device(): gathered = lax.all_gather(gathered, ('x', 'y', 'c'), axis=0, tiled=True)  36.7 us
    all_gather x1, blocking collectives, per_device(): gathered = lax.all_gather(loadings, 'zh', axis=0, tiled=True)  20.3 us
    all_to_all x1, waiting for transfers between devices, per_device(): lax.all_to_all(sent.reshape(owners, per, terms + 2), 'trade', 0, 0, tiled...  17.1 us
    all_to_all x1, blocking collectives, per_device(): lax.all_to_all(partial_cp.reshape(rows, owners, CP_DEV), 'trade', 1, 1, t...  15.6 us
    all_to_all x1, starting transfers between devices, per_device(): lax.all_to_all(sent.reshape(owners, per, terms + 2), 'trade', 0, 0, tiled...  13.6 us
    dot_general x1, matrix products, per_device(): jnp.dot(factors, pick, preferred_element_type=jnp.float32)  8.71 us
  transfers between devices with their start and end apart: 2, of which 2 were waited for; matrix products, arithmetic and copies ran while one was open for 4% of the time, Pallas kernels for 0%

profile of v5, /device:TPU:6, one launch (start us, length us, event | category | flops | bytes accessed | tf_op | source)
XLA Modules:
  0.0 174.6 jit_solution(16593474492878260077)
XLA Ops:
  6.5 0.0 copy-start
  6.5 0.0 all-gather.2.cloned.1.call-start
  6.5 20.3 %all_gather.6 = bf16[128,1024]{1,0:T(8,128)(2,1)} all-gather(bf16[64,1024]{1,0:T(8,128)(2,1)} %param.8), channel_id=1, replica_groups=mesh['x'=4,'zh'=2,'y'=4,'c'=2,'trade'=8] {'zh'}, dimensions={0}, use_global_device_ids=true | all-gather | bytes 393216 | tf_op jit(solution)/shard_map/all_gather | solution.py:69
  26.8 0.0 all-gather.2.cloned.1.call-update
  26.8 0.9 convert_element_type.66
  27.7 0.7 convert_element_type.68
  28.4 0.7 add_select_fusion.1
  29.1 0.5 fusion.14
  29.6 0.7 fusion.40
  30.3 1.7 fusion.2
  32.1 0.1 copy.24
  32.1 0.0 copy-start.2
  32.2 0.8 copy.16
  33.0 13.6 %all-to-all-start = ((f32[8,128,66]{1,2,0:T(8,128)}), f32[8,128,66]{1,2,0:T(8,128)S(1)}, u32[]{:S(2)}, u32[]{:S(2)}) async-start(f32[8,128,66]{1,2,0:T(8,128)} %copy.16), calls=%async_computation | async-start | bytes 589824 | tf_op jit(solution)/shard_map/all_to_all | solution.py:63
  46.5 0.0 copy-done
  46.5 0.7 copy.18
  47.2 0.1 copy.19
  47.3 17.1 %all-to-all-done = f32[8,128,66]{1,2,0:T(8,128)S(1)} async-done(((f32[8,128,66]{1,2,0:T(8,128)}), f32[8,128,66]{1,2,0:T(8,128)S(1)}, u32[]{:S(2)}, u32[]{:S(2)}) %all-to-all-start) | async-done | bytes 270368 | tf_op jit(solution)/shard_map/all_to_all | solution.py:63
  64.4 0.1 copy.29
  64.5 0.1 copy.25
  64.7 0.1 fusion.47
  64.7 0.1 fusion.45
  64.8 0.1 fusion.46
  64.9 36.7 %all-gather.2.cloned.1.call-done = bf16[4096,1024]{1,0:T(8,128)(2,1)} async-done(((bf16[128,1024]{1,0:T(8,128)(2,1)}), bf16[4096,1024]{1,0:T(8,128)(2,1)}) %all-gather.2.cloned.1.call-update) | async-done | bytes 8388624 | tf_op jit(solution)/shard_map/all_gather | solution.py:70
  101.6 0.0 copy-done.2
  101.6 8.7 %subtract_convert_fusion = bf16[128,1024]{1,0:T(8,128)(2,1)S(1)} fusion(s32[1024]{0:T(1024)S(1)} %bitcast.173, bf16[128,4096]{0,1:T(8,128)(2,1)S(1)} %bitcast.101, bf16[4096,1024]{1,0:T(8,128)(2,1)} %all-gather.2.cloned.1.call-done, bf16[128,1024]{1,0:T(8,128)(2,1)S(1)} %copy-done.2, f32[1024]{0:T(1024)S(1)} %bitcast.134, f32[1024]{0:T(1024)S(1)} %bitcast.135, ...), kind=kOutput, calls=%fused_computation.22 | convolution fusion | flops 1369178112 | bytes 10227712 | tf_op jit(solution)/shard_map/dot_general | solution.py:78
  110.3 0.0 copy-start.1
  110.3 1.9 %fusion.5 = bf16[128,2048]{1,0:T(8,128)(2,1)S(1)} fusion(bf16[128,1024]{1,0:T(8,128)(2,1)S(1)} %subtract_convert_fusion, s32[1024]{0:T(1024)S(1)} %bitcast.172), kind=kOutput, calls=%fused_computation.9 | convolution fusion | flops 539230208 | bytes 790528 | tf_op jit(solution)/shard_map/dot_general | solution.py:85
  112.2 38.9 %all_to_all.15 = bf16[128,8,256]{2,0,1:T(8,128)(2,1)S(1)} all-to-all(bf16[128,8,256]{2,0,1:T(8,128)(2,1)S(1)} %bitcast.97), channel_id=1, replica_groups=mesh['x'=4,'zh'=2,'y'=4,'c'=2,'trade'=8] {'trade'}, dimensions={1} | all-to-all | bytes 1048576 | tf_op jit(solution)/shard_map/all_to_all | solution.py:87
  151.2 0.1 convert_reduce_fusion
  151.2 0.0 copy-done.1
  151.2 0.3 fusion.35
  151.6 15.6 %all_to_all.16 = f32[128,8,32]{0,2,1:T(8,128)S(1)} all-to-all(f32[128,8,32]{0,2,1:T(8,128)S(1)} %bitcast.105), channel_id=1, replica_groups=mesh['x'=4,'zh'=2,'y'=4,'c'=2,'trade'=8] {'trade'}, dimensions={1} | all-to-all | bytes 262144 | tf_op jit(solution)/shard_map/all_to_all | solution.py:93
  167.1 0.6 reduce_sum.29
  (6 shorter events, 0.1 us)
Async XLA Ops:
  6.5 40.0 %copy-start = (bf16[128,4096]{1,0:T(8,128)(2,1)S(1)}, bf16[128,4096]{1,0:T(8,128)(2,1)}, u32[]{:S(2)}) copy-start(bf16[128,4096]{1,0:T(8,128)(2,1)} %param.7) | copy-start | bytes 3145732
  6.5 95.0 %all-gather.2.cloned.1.call-start = ((), (), s32[]{:S(2)}) async-start(), calls=%async_computation.3 | async-start | bytes 8650752 | tf_op jit(solution)/shard_map/all_gather | solution.py:70
  32.1 69.4 %copy-start.2 = (bf16[128,1024]{1,0:T(8,128)(2,1)S(1)}, bf16[128,1024]{1,0:T(8,128)(2,1)}, u32[]{:S(2)}) copy-start(bf16[128,1024]{1,0:T(8,128)(2,1)} %param.9) | copy-start | bytes 786436
  33.0 31.5 %all-to-all-start = ((f32[8,128,66]{1,2,0:T(8,128)}), f32[8,128,66]{1,2,0:T(8,128)S(1)}, u32[]{:S(2)}, u32[]{:S(2)}) async-start(f32[8,128,66]{1,2,0:T(8,128)} %copy.16), calls=%async_computation | async-start | bytes 589824 | tf_op jit(solution)/shard_map/all_to_all | solution.py:63
  110.3 41.0 %copy-start.1 = (s32[256]{0:T(256)S(1)}, s32[256]{0:T(256)}, u32[]{:S(2)}) copy-start(s32[256]{0:T(256)} %param.13) | copy-start | bytes 3076
Sparse Core Ops, SparseCore 0:
  26.9 74.5 all-gather.1

commit v6 on v5

--- a/solution.py
+++ b/solution.py
@@ -66,14 +66,21 @@
     got_col = got[:, terms].astype(jnp.int32)
     got_ns = got[:, terms + 1].astype(jnp.int32)
 
-    gathered = lax.all_gather(loadings, "zh", axis=0, tiled=True)
-    gathered = lax.all_gather(gathered, ("x", "y", "c"), axis=0, tiled=True)
     rows = drivers.shape[0]
     lead = loadings.shape[0]
     sizes = [lax.axis_size(name) for name in PATH]
-    order = drivers.reshape(rows, *sizes, lead).transpose(0, 1, 3, 4, 2, 5).reshape(rows, -1)
+    cores = sizes[3]
+    half = width // cores
+    mine = lax.all_to_all(loadings.reshape(lead, cores, half), "c", 1, 0, tiled=False)
+    gathered = lax.all_gather(mine.reshape(cores * lead, half), "zh", axis=0, tiled=True)
+    gathered = lax.all_gather(gathered, ("x", "y"), axis=0, tiled=True)
+    both = lax.all_gather(drivers, "c", axis=0, tiled=True)
+    order = both.reshape(cores * rows, *sizes, lead).transpose(0, 1, 3, 2, 4, 5).reshape(cores * rows, -1)
     moved = jnp.dot(order, gathered, preferred_element_type=jnp.float32)
-    factors = (start_state.astype(jnp.float32) + moved).astype(jnp.bfloat16)
+    before = lax.all_to_all(start_state.reshape(rows, cores, half), "c", 1, 0, tiled=False)
+    halves = (before.reshape(cores * rows, half).astype(jnp.float32) + moved).astype(jnp.bfloat16)
+    back = lax.all_to_all(halves.reshape(cores, rows, half), "c", 0, 1, tiled=False)
+    factors = back.reshape(rows, width)
     pick = (jnp.arange(width, dtype=jnp.int32)[:, None] == got_col[None, :]).astype(jnp.bfloat16)
     chosen = jnp.dot(factors, pick, preferred_element_type=jnp.float32).astype(jnp.bfloat16)
     values = clenshaw(chosen, got_coeffs.astype(jnp.float32).T)

time: 175 us -> 184 us (1.051)
  blocking collectives: 74.8 us -> 80.9 us
  local copies, waits for them, and re-layouts: 2 us -> 7.46 us
  starting transfers between devices: 13.6 us -> 18.8 us
  waiting for transfers between devices: 53.9 us -> 50.3 us
  other arithmetic: 3.73 us -> 0.81 us
    all_to_all x0 -> x2, blocking collectives: none -> 7.78 us  [the longest x1 3.94 us: per_device(): lax.all_to_all(halves.reshape(cores, rows, half), 'c', 0, 1, tiled=False)]
    dot_general x1, matrix products: 8.71 us -> 3.45 us  [per_device(): moved = jnp.dot(order, gathered, preferred_element_type=jnp.float32)]
    dot_general x1, matrix products: 1.89 us -> 6.1 us  [per_device(): netting = jnp.dot(values, net_table, preferred_element_type=jnp.float32)]
    all_gather x1 -> x2, waiting for transfers between devices: 36.7 us -> 33 us  [the longest x1 33 us: per_device(): gathered = lax.all_gather(gathered, ('x', 'y'), axis=0, tiled=True)]
    all_to_all x0 -> x1, starting transfers between devices: none -> 3.44 us  [per_device(): lax.all_to_all(start_state.reshape(rows, cores, half), 'c', 1, 0, tiled=F...]
    another operation x0 -> x4, local copies, waits for them, and re-layouts: none -> 2.04 us  [the longest x2 1 us: per_device(): lax.all_to_all(loadings.reshape(lead, cores, half), 'c', 1, 0, tiled=False)]
  transfers between devices with their start and end apart: 2 -> 4, of which waited for: 2 -> 2; matrix products, arithmetic and copies ran while one was open for 4% -> 4% of each run, Pallas kernels for 0% -> 0%
where the time goes in v6:
time: 184 us
  blocking collectives  80.9 us (44%)
  waiting for transfers between devices  50.3 us (27%)
  starting transfers between devices  18.8 us (10%)
  between operations  13.6 us (7%)
  matrix products  12.1 us (7%)
  local copies, waits for them, and re-layouts  7.46 us (4%)
    all_to_all x1, blocking collectives, per_device(): lax.all_to_all(sent, 'trade', 1, 1, tiled=False).astype(jnp.float32)  38.8 us
    all_gather x1, waiting for transfers between devices, per_device(): gathered = lax.all_gather(gathered, ('x', 'y'), axis=0, tiled=True)  33 us
    all_gather x1, blocking collectives, per_device(): lax.all_gather(mine.reshape(cores * lead, half), 'zh', axis=0, tiled=True)  18.7 us
    all_to_all x1, waiting for transfers between devices, per_device(): lax.all_to_all(sent.reshape(owners, per, terms + 2), 'trade', 0, 0, tiled...  17.3 us
    all_to_all x1, blocking collectives, per_device(): lax.all_to_all(partial_cp.reshape(rows, owners, CP_DEV), 'trade', 1, 1, t...  15.6 us
    all_to_all x1, starting transfers between devices, per_device(): lax.all_to_all(sent.reshape(owners, per, terms + 2), 'trade', 0, 0, tiled...  15.2 us
    dot_general x1, matrix products, per_device(): netting = jnp.dot(values, net_table, preferred_element_type=jnp.float32)  6.1 us
    all_to_all x1, blocking collectives, per_device(): lax.all_to_all(halves.reshape(cores, rows, half), 'c', 0, 1, tiled=False)  3.94 us
  transfers between devices with their start and end apart: 4, of which 2 were waited for; matrix products, arithmetic and copies ran while one was open for 4% of the time, Pallas kernels for 0%

profile of v6, /device:TPU:6, one launch (start us, length us, event | category | flops | bytes accessed | tf_op | source)
XLA Modules:
  0.0 183.9 jit_solution(3543611825917913098)
XLA Ops:
  6.5 0.0 copy-start
  6.5 0.0 copy-start.1
  6.5 0.0 copy-start.3
  6.5 0.0 copy-start.2
  6.5 0.0 all-gather.3.cloned.1.call-start
  6.6 2.3 %copy.31 = bf16[128,4096]{0,1:T(8,128)(2,1)} copy(bf16[128,4096]{1,0:T(8,128)(2,1)} %param.7) | data formatting | bytes 2097152 | tf_op args[0]
  8.9 0.0 all-gather.3.cloned.1.call-update
  8.9 0.0 all-gather.5.cloned.1.call-start
  9.0 1.0 broadcast_in_dim_reshape.10
  10.0 3.8 %all_to_all.54 = bf16[1,64,2,512]{3,1,0,2:T(8,128)(2,1)S(1)} all-to-all(bf16[1,64,2,512]{3,1,0,2:T(8,128)(2,1)S(1)} %copy.33), channel_id=1, replica_groups=mesh['x'=4,'zh'=2,'y'=4,'c'=2,'trade'=8] {'c'}, dimensions={2} | all-to-all | bytes 262144 | tf_op jit(solution)/shard_map/all_to_all | solution.py:74
  13.8 18.7 %all_gather.10 = bf16[256,512]{1,0:T(8,128)(2,1)} all-gather(bf16[128,512]{1,0:T(8,128)(2,1)S(1)} %bitcast.123), channel_id=1, replica_groups=mesh['x'=4,'zh'=2,'y'=4,'c'=2,'trade'=8] {'zh'}, dimensions={0}, use_global_device_ids=true | all-gather | bytes 393216 | tf_op jit(solution)/shard_map/all_gather | solution.py:75
  32.5 0.0 all-gather.5.cloned.1.call-update
  32.5 0.0 copy-done
  32.5 0.2 copy.29
  32.7 0.9 copy.30
  33.6 3.4 %all-to-all-start.1 = ((bf16[1,128,2,512]{3,1,0,2:T(8,128)(2,1)}), bf16[1,128,2,512]{3,1,0,2:T(8,128)(2,1)S(1)}, u32[]{:S(2)}, u32[]{:S(2)}) async-start(bf16[1,128,2,512]{3,1,0,2:T(8,128)(2,1)} %copy.30), calls=%async_computation.1 | async-start | bytes 524288 | tf_op jit(solution)/shard_map/all_to_all | solution.py:80
  37.0 0.0 copy-done.1
  37.1 0.0 copy-done.3
  37.1 0.0 copy-done.2
  37.1 0.5 fusion.14
  37.6 1.7 fusion.2
  39.3 0.1 copy.39
  39.4 0.8 copy.27
  40.2 0.0 all-to-all-done.1
  40.2 15.2 %all-to-all-start = ((f32[8,128,66]{1,2,0:T(8,128)}), f32[8,128,66]{1,2,0:T(8,128)S(1)}, u32[]{:S(2)}, u32[]{:S(2)}) async-start(f32[8,128,66]{1,2,0:T(8,128)} %copy.27), calls=%async_computation | async-start | bytes 589824 | tf_op jit(solution)/shard_map/all_to_all | solution.py:63
  55.5 17.3 %all-to-all-done = f32[8,128,66]{1,2,0:T(8,128)S(1)} async-done(((f32[8,128,66]{1,2,0:T(8,128)}), f32[8,128,66]{1,2,0:T(8,128)S(1)}, u32[]{:S(2)}, u32[]{:S(2)}) %all-to-all-start) | async-done | bytes 270368 | tf_op jit(solution)/shard_map/all_to_all | solution.py:63
  72.8 0.1 copy.44
  72.9 0.1 copy.40
  73.0 0.1 fusion.113
  73.1 0.1 fusion.114
  73.2 0.1 fusion.112
  73.2 0.0 all-gather.3.cloned.1.call-done
  73.3 1.7 copy.32
  75.0 33.0 %all-gather.5.cloned.1.call-done = bf16[4096,512]{1,0:T(8,128)(2,1)} async-done(((bf16[256,512]{1,0:T(8,128)(2,1)}), bf16[4096,512]{1,0:T(8,128)(2,1)}) %all-gather.5.cloned.1.call-update) | async-done | bytes 4194320 | tf_op jit(solution)/shard_map/all_gather | solution.py:76
  108.0 3.4 %fusion.8 = bf16[256,512]{1,0:T(8,128)(2,1)S(1)} fusion(f32[256,512]{1,0:T(8,128)S(1)} %bitcast.124, bf16[256,4096]{0,1:T(8,128)(2,1)S(1)} %bitcast.115, bf16[4096,512]{1,0:T(8,128)(2,1)} %all-gather.5.cloned.1.call-done), kind=kOutput, calls=%fused_computation.13 | convolution fusion | flops 1074003968 | bytes 7077888 | tf_op jit(solution)/shard_map/dot_general | solution.py:79
  111.4 0.2 copy.34
  111.6 3.9 %all_to_all.55 = bf16[2,128,1,512]{1,3,2,0:T(8,128)(2,1)S(1)} all-to-all(bf16[2,128,1,512]{1,3,2,0:T(8,128)(2,1)S(1)} %copy.34), channel_id=1, replica_groups=mesh['x'=4,'zh'=2,'y'=4,'c'=2,'trade'=8] {'c'}, dimensions={0} | all-to-all | bytes 524288 | tf_op jit(solution)/shard_map/all_to_all | solution.py:82
  115.5 0.0 copy-start.4
  115.5 6.1 %fusion.5 = bf16[128,2048]{1,0:T(8,128)(2,1)S(1)} fusion(s32[1024]{0:T(1024)S(1)} %bitcast.196, bf16[128,1024]{0,1:T(8,128)(2,1)S(1)} %bitcast.128, s32[1024]{0:T(1024)S(1)} %bitcast.195, f32[1024]{0:T(1024)S(1)} %bitcast.176, f32[1024]{0:T(1024)S(1)} %bitcast.177, f32[1024]{0:T(1024)S(1)} %bitcast.178, f32[1024]{0:T(1024)S(1)} %bitcast.179, ...), kind=kOutput, calls=%fused_computation.9 | convolution fusion | flops 834273280 | bytes 1056768 | tf_op jit(solution)/shard_map/dot_general | solution.py:92
  121.7 38.8 %all_to_all.56 = bf16[128,8,256]{2,0,1:T(8,128)(2,1)S(1)} all-to-all(bf16[128,8,256]{2,0,1:T(8,128)(2,1)S(1)} %bitcast.116), channel_id=1, replica_groups=mesh['x'=4,'zh'=2,'y'=4,'c'=2,'trade'=8] {'trade'}, dimensions={1} | all-to-all | bytes 1048576 | tf_op jit(solution)/shard_map/all_to_all | solution.py:94
  160.5 0.1 convert_reduce_fusion
  160.6 0.0 copy-done.4
  160.6 0.3 fusion.100
  160.9 15.6 %all_to_all.57 = f32[128,8,32]{0,2,1:T(8,128)S(1)} all-to-all(f32[128,8,32]{0,2,1:T(8,128)S(1)} %bitcast.126), channel_id=1, replica_groups=mesh['x'=4,'zh'=2,'y'=4,'c'=2,'trade'=8] {'trade'}, dimensions={1} | all-to-all | bytes 262144 | tf_op jit(solution)/shard_map/all_to_all | solution.py:100
  176.5 0.6 reduce_sum.29
  (12 shorter events, 0.2 us)
Async XLA Ops:
  6.5 26.0 %copy-start = (bf16[128,1024]{1,0:T(8,128)(2,1)S(1)}, bf16[128,1024]{1,0:T(8,128)(2,1)}, u32[]{:S(2)}) copy-start(bf16[128,1024]{1,0:T(8,128)(2,1)} %param.9) | copy-start | bytes 786436
  6.5 30.5 %copy-start.1 = (bf16[1024,64]{0,1:T(8,128)(2,1)S(1)}, bf16[1024,64]{0,1:T(8,128)(2,1)}, u32[]{:S(2)}) copy-start(bf16[1024,64]{0,1:T(8,128)(2,1)} %param.10) | copy-start | bytes 393220
  6.5 30.5 %copy-start.3 = (s32[1024]{0:T(1024)S(1)}, s32[1024]{0:T(1024)}, u32[]{:S(2)}) copy-start(s32[1024]{0:T(1024)} %param.12) | copy-start | bytes 12292
  6.5 30.5 %copy-start.2 = (s32[1024]{0:T(1024)S(1)}, s32[1024]{0:T(1024)}, u32[]{:S(2)}) copy-start(s32[1024]{0:T(1024)} %param.11) | copy-start | bytes 12292
  6.5 66.7 %all-gather.3.cloned.1.call-start = ((), (), s32[]{:S(2)}) async-start(), calls=%async_computation.6 | async-start | bytes 3145728 | tf_op jit(solution)/shard_map/all_gather | solution.py:77
  8.9 99.1 %all-gather.5.cloned.1.call-start = ((), (), s32[]{:S(2)}) async-start(), calls=%async_computation.7 | async-start | bytes 4456448 | tf_op jit(solution)/shard_map/all_gather | solution.py:76
  33.6 6.6 %all-to-all-start.1 = ((bf16[1,128,2,512]{3,1,0,2:T(8,128)(2,1)}), bf16[1,128,2,512]{3,1,0,2:T(8,128)(2,1)S(1)}, u32[]{:S(2)}, u32[]{:S(2)}) async-start(bf16[1,128,2,512]{3,1,0,2:T(8,128)(2,1)} %copy.30), calls=%async_computation.1 | async-start | bytes 524288 | tf_op jit(solution)/shard_map/all_to_all | solution.py:80
  40.2 32.6 %all-to-all-start = ((f32[8,128,66]{1,2,0:T(8,128)}), f32[8,128,66]{1,2,0:T(8,128)S(1)}, u32[]{:S(2)}, u32[]{:S(2)}) async-start(f32[8,128,66]{1,2,0:T(8,128)} %copy.27), calls=%async_computation | async-start | bytes 589824 | tf_op jit(solution)/shard_map/all_to_all | solution.py:63
  115.5 45.0 %copy-start.4 = (s32[256]{0:T(256)S(1)}, s32[256]{0:T(256)}, u32[]{:S(2)}) copy-start(s32[256]{0:T(256)} %param.13) | copy-start | bytes 3076
Sparse Core Ops, SparseCore 0:
  9.4 24.9 all-gather.2
  37.5 70.4 all-gather.4

commit v7 on v5

--- a/solution.py
+++ b/solution.py
@@ -90,7 +90,8 @@
         jnp.bfloat16
     )
     partial_cp = jnp.dot(positive, cp_table, preferred_element_type=jnp.float32)
-    pieces = lax.all_to_all(partial_cp.reshape(rows, owners, CP_DEV), "trade", 1, 1, tiled=False)
+    sent_cp = partial_cp.astype(jnp.bfloat16).reshape(rows, owners, CP_DEV)
+    pieces = lax.all_to_all(sent_cp, "trade", 1, 1, tiled=False).astype(jnp.float32)
     return jnp.sum(pieces, axis=1).T
 
 

time: 175 us -> 175 us (level)
  no operation moved by 1% of the time
where the time goes in v7:
time: 175 us; the launch traced here: 174 us
  blocking collectives  74.1 us (42%)
  waiting for transfers between devices  53.9 us (31%)
  starting transfers between devices  13.6 us (8%)
  between operations  13.6 us (8%)
  matrix products  13 us (7%)
  other arithmetic  3.73 us (2%)
  local copies, waits for them, and re-layouts  2.12 us (1%)
    all_to_all x1, blocking collectives, per_device(): lax.all_to_all(sent, 'trade', 1, 1, tiled=False).astype(jnp.float32)  38.9 us
    all_gather x1, waiting for transfers between devices, per_device(): gathered = lax.all_gather(gathered, ('x', 'y', 'c'), axis=0, tiled=True)  36.7 us
    all_gather x1, blocking collectives, per_device(): gathered = lax.all_gather(loadings, 'zh', axis=0, tiled=True)  20.3 us
    all_to_all x1, waiting for transfers between devices, per_device(): lax.all_to_all(sent.reshape(owners, per, terms + 2), 'trade', 0, 0, tiled...  17.1 us
    all_to_all x1, blocking collectives, per_device(): lax.all_to_all(sent_cp, 'trade', 1, 1, tiled=False).astype(jnp.float32)  15 us
    all_to_all x1, starting transfers between devices, per_device(): lax.all_to_all(sent.reshape(owners, per, terms + 2), 'trade', 0, 0, tiled...  13.6 us
    dot_general x1, matrix products, per_device(): jnp.dot(factors, pick, preferred_element_type=jnp.float32)  8.71 us
  transfers between devices with their start and end apart: 2, of which 2 were waited for; matrix products, arithmetic and copies ran while one was open for 4% of the time, Pallas kernels for 0%

profile of v7, /device:TPU:6, one launch (start us, length us, event | category | flops | bytes accessed | tf_op | source)
XLA Modules:
  0.0 174.0 jit_solution(8284468715830699999)
XLA Ops:
  6.5 0.0 copy-start
  6.5 0.0 all-gather.2.cloned.1.call-start
  6.5 20.3 %all_gather.6 = bf16[128,1024]{1,0:T(8,128)(2,1)} all-gather(bf16[64,1024]{1,0:T(8,128)(2,1)} %param.8), channel_id=1, replica_groups=mesh['x'=4,'zh'=2,'y'=4,'c'=2,'trade'=8] {'zh'}, dimensions={0}, use_global_device_ids=true | all-gather | bytes 393216 | tf_op jit(solution)/shard_map/all_gather | solution.py:69
  26.8 0.0 all-gather.2.cloned.1.call-update
  26.8 0.9 convert_element_type.72
  27.7 0.7 convert_element_type.74
  28.4 0.7 add_select_fusion.1
  29.1 0.5 fusion.14
  29.6 0.7 fusion.39
  30.3 1.7 fusion.2
  32.1 0.1 copy.23
  32.1 0.0 copy-start.1
  32.2 0.8 copy.16
  33.0 13.6 %all-to-all-start = ((f32[8,128,66]{1,2,0:T(8,128)}), f32[8,128,66]{1,2,0:T(8,128)S(1)}, u32[]{:S(2)}, u32[]{:S(2)}) async-start(f32[8,128,66]{1,2,0:T(8,128)} %copy.16), calls=%async_computation | async-start | bytes 589824 | tf_op jit(solution)/shard_map/all_to_all | solution.py:63
  46.5 0.0 copy-done
  46.5 0.7 copy.18
  47.2 0.1 copy.19
  47.3 17.1 %all-to-all-done = f32[8,128,66]{1,2,0:T(8,128)S(1)} async-done(((f32[8,128,66]{1,2,0:T(8,128)}), f32[8,128,66]{1,2,0:T(8,128)S(1)}, u32[]{:S(2)}, u32[]{:S(2)}) %all-to-all-start) | async-done | bytes 270368 | tf_op jit(solution)/shard_map/all_to_all | solution.py:63
  64.4 0.1 copy.28
  64.5 0.1 copy.24
  64.7 0.1 fusion.46
  64.7 0.1 fusion.44
  64.8 0.1 fusion.45
  64.9 36.7 %all-gather.2.cloned.1.call-done = bf16[4096,1024]{1,0:T(8,128)(2,1)} async-done(((bf16[128,1024]{1,0:T(8,128)(2,1)}), bf16[4096,1024]{1,0:T(8,128)(2,1)}) %all-gather.2.cloned.1.call-update) | async-done | bytes 8388624 | tf_op jit(solution)/shard_map/all_gather | solution.py:70
  101.6 0.0 copy-done.1
  101.6 8.7 %subtract_convert_fusion = bf16[128,1024]{1,0:T(8,128)(2,1)S(1)} fusion(s32[1024]{0:T(1024)S(1)} %bitcast.173, bf16[128,4096]{0,1:T(8,128)(2,1)S(1)} %bitcast.101, bf16[4096,1024]{1,0:T(8,128)(2,1)} %all-gather.2.cloned.1.call-done, bf16[128,1024]{1,0:T(8,128)(2,1)S(1)} %copy-done.1, f32[1024]{0:T(1024)S(1)} %bitcast.134, f32[1024]{0:T(1024)S(1)} %bitcast.135, ...), kind=kOutput, calls=%fused_computation.23 | convolution fusion | flops 1369178112 | bytes 10227712 | tf_op jit(solution)/shard_map/dot_general | solution.py:78
  110.3 0.0 copy-start.2
  110.3 1.9 %fusion.5 = bf16[128,2048]{1,0:T(8,128)(2,1)S(1)} fusion(bf16[128,1024]{1,0:T(8,128)(2,1)S(1)} %subtract_convert_fusion, s32[1024]{0:T(1024)S(1)} %bitcast.172), kind=kOutput, calls=%fused_computation.9 | convolution fusion | flops 539230208 | bytes 790528 | tf_op jit(solution)/shard_map/dot_general | solution.py:85
  112.2 38.9 %all_to_all.15 = bf16[128,8,256]{2,0,1:T(8,128)(2,1)S(1)} all-to-all(bf16[128,8,256]{2,0,1:T(8,128)(2,1)S(1)} %bitcast.97), channel_id=1, replica_groups=mesh['x'=4,'zh'=2,'y'=4,'c'=2,'trade'=8] {'trade'}, dimensions={1} | all-to-all | bytes 1048576 | tf_op jit(solution)/shard_map/all_to_all | solution.py:87
  151.2 0.1 convert_reduce_fusion
  151.2 0.0 copy-done.2
  151.2 0.2 convolution_convert_fusion
  151.5 0.1 copy.21
  151.6 15.0 %all_to_all.16 = bf16[128,8,32]{0,2,1:T(8,128)(2,1)S(1)} all-to-all(bf16[128,8,32]{0,2,1:T(8,128)(2,1)S(1)} %bitcast.106), channel_id=1, replica_groups=mesh['x'=4,'zh'=2,'y'=4,'c'=2,'trade'=8] {'trade'}, dimensions={1} | all-to-all | bytes 131072 | tf_op jit(solution)/shard_map/all_to_all | solution.py:94
  166.6 0.6 convert_reduce_fusion.1
  (6 shorter events, 0.1 us)
Async XLA Ops:
  6.5 40.0 %copy-start = (bf16[128,4096]{1,0:T(8,128)(2,1)S(1)}, bf16[128,4096]{1,0:T(8,128)(2,1)}, u32[]{:S(2)}) copy-start(bf16[128,4096]{1,0:T(8,128)(2,1)} %param.7) | copy-start | bytes 3145732
  6.5 95.0 %all-gather.2.cloned.1.call-start = ((), (), s32[]{:S(2)}) async-start(), calls=%async_computation.3 | async-start | bytes 8650752 | tf_op jit(solution)/shard_map/all_gather | solution.py:70
  32.1 69.4 %copy-start.1 = (bf16[128,1024]{1,0:T(8,128)(2,1)S(1)}, bf16[128,1024]{1,0:T(8,128)(2,1)}, u32[]{:S(2)}) copy-start(bf16[128,1024]{1,0:T(8,128)(2,1)} %param.9) | copy-start | bytes 786436
  33.0 31.5 %all-to-all-start = ((f32[8,128,66]{1,2,0:T(8,128)}), f32[8,128,66]{1,2,0:T(8,128)S(1)}, u32[]{:S(2)}, u32[]{:S(2)}) async-start(f32[8,128,66]{1,2,0:T(8,128)} %copy.16), calls=%async_computation | async-start | bytes 589824 | tf_op jit(solution)/shard_map/all_to_all | solution.py:63
  110.3 41.0 %copy-start.2 = (s32[256]{0:T(256)S(1)}, s32[256]{0:T(256)}, u32[]{:S(2)}) copy-start(s32[256]{0:T(256)} %param.13) | copy-start | bytes 3076
Sparse Core Ops, SparseCore 0:
  26.9 74.5 all-gather.1

commit v8 on v5

--- a/solution.py
+++ b/solution.py
@@ -48,6 +48,19 @@
     return acc
 
 
+def across_planes(block):
+    planes = lax.axis_size("zh")
+    owners = lax.axis_size("trade")
+    ring = planes * owners
+    split = block.shape[1] // 2
+    straight = lax.ppermute(block[:, :split], "zh", [(z, (z + 1) % planes) for z in range(planes)])
+    back = [(z, (z - ring // 4) % ring) for z in range(ring)]
+    relayed = lax.ppermute(lax.ppermute(block[:, split:], ("zh", "trade"), back), ("zh", "trade"), back)
+    partner = jnp.concatenate([straight, relayed], axis=1)
+    first = lax.axis_index("zh") == 0
+    return jnp.where(first, jnp.concatenate([block, partner]), jnp.concatenate([partner, block]))
+
+
 def per_device(drivers, loadings, start_state, coeffs, trade_col, trade_ns, ns_cp):
     owners = lax.axis_size("trade")
     width = start_state.shape[1]
@@ -66,7 +79,7 @@
     got_col = got[:, terms].astype(jnp.int32)
     got_ns = got[:, terms + 1].astype(jnp.int32)
 
-    gathered = lax.all_gather(loadings, "zh", axis=0, tiled=True)
+    gathered = across_planes(loadings)
     gathered = lax.all_gather(gathered, ("x", "y", "c"), axis=0, tiled=True)
     rows = drivers.shape[0]
     lead = loadings.shape[0]

time: 175 us -> 183 us (1.046)
  blocking collectives: 74.8 us -> 54.5 us
  starting transfers between devices: 13.6 us -> 30.7 us
  waiting for transfers between devices: 53.9 us -> 60.9 us
    ppermute x0 -> x3, starting transfers between devices: none -> 26.1 us  [the longest x1 12.7 us: across_planes(): lax.ppermute(block[:, split:], ('zh', 'trade'), back)]
    all_gather x1 -> x0, blocking collectives: 20.3 us -> none  [per_device(): gathered = lax.all_gather(loadings, 'zh', axis=0, tiled=True)]
    ppermute x0 -> x3, waiting for transfers between devices: none -> 9.49 us  [the longest x1 7.94 us: across_planes(): lax.ppermute(lax.ppermute(block[:, split:], ('zh', 'trade'), back), ('zh'...]
    all_to_all x1, starting transfers between devices: 13.6 us -> 4.6 us  [per_device(): lax.all_to_all(sent.reshape(owners, per, terms + 2), 'trade', 0, 0, tiled...]
    all_gather x1, waiting for transfers between devices: 36.7 us -> 34.4 us  [per_device(): gathered = lax.all_gather(gathered, ('x', 'y', 'c'), axis=0, tiled=True)]
  transfers between devices with their start and end apart: 2 -> 5, of which waited for: 2 -> 5; matrix products, arithmetic and copies ran while one was open for 4% -> 4% of each run, Pallas kernels for 0% -> 0%
where the time goes in v8:
time: 183 us
  waiting for transfers between devices  60.9 us (33%)
  blocking collectives  54.5 us (30%)
  starting transfers between devices  30.7 us (17%)
  matrix products  14.2 us (8%)
  between operations  13.6 us (7%)
  other arithmetic  5.54 us (3%)
  local copies, waits for them, and re-layouts  3.16 us (2%)
    all_to_all x1, blocking collectives, per_device(): lax.all_to_all(sent, 'trade', 1, 1, tiled=False).astype(jnp.float32)  38.9 us
    all_gather x1, waiting for transfers between devices, per_device(): gathered = lax.all_gather(gathered, ('x', 'y', 'c'), axis=0, tiled=True)  34.4 us
    all_to_all x1, waiting for transfers between devices, per_device(): lax.all_to_all(sent.reshape(owners, per, terms + 2), 'trade', 0, 0, tiled...  17.1 us
    all_to_all x1, blocking collectives, per_device(): lax.all_to_all(partial_cp.reshape(rows, owners, CP_DEV), 'trade', 1, 1, t...  15.6 us
    ppermute x1, starting transfers between devices, across_planes(): lax.ppermute(block[:, split:], ('zh', 'trade'), back)  12.7 us
    dot_general x1, matrix products, per_device(): jnp.dot(factors, pick, preferred_element_type=jnp.float32)  9.74 us
    ppermute x1, starting transfers between devices, across_planes(): lax.ppermute(lax.ppermute(block[:, split:], ('zh', 'trade'), back), ('zh'...  8.41 us
    ppermute x1, waiting for transfers between devices, across_planes(): lax.ppermute(lax.ppermute(block[:, split:], ('zh', 'trade'), back), ('zh'...  7.94 us
  transfers between devices with their start and end apart: 5, of which 5 were waited for; matrix products, arithmetic and copies ran while one was open for 4% of the time, Pallas kernels for 0%

profile of v8, /device:TPU:6, one launch (start us, length us, event | category | flops | bytes accessed | tf_op | source)
XLA Modules:
  0.0 182.5 jit_solution(4593796262144258879)
XLA Ops:
  6.5 0.0 copy-start
  6.5 0.0 all-gather.2.cloned.1.call-start
  6.5 1.0 fusion.50
  7.5 12.7 %collective-permute-start.1 = (bf16[64,512]{1,0:T(8,128)(2,1)S(1)}, bf16[64,512]{1,0:T(8,128)(2,1)S(1)}, u32[]{:S(2)}, u32[]{:S(2)}) collective-permute-start(bf16[64,512]{1,0:T(8,128)(2,1)S(1)} %get-tuple-element.71), channel_id=1, source_target_pairs={{0,68},{1,69},{2,70},{3,71},{4,0},{5,1},{6,2},{7,3},{64,4},{65,5},... | collective-permute-start | bytes 196616 | tf_op jit(solution)/shard_map/ppermute | solution.py:58
  20.3 4.9 %collective-permute-start = (bf16[64,512]{1,0:T(8,128)(2,1)S(1)}, bf16[64,512]{1,0:T(8,128)(2,1)S(1)}, u32[]{:S(2)}, u32[]{:S(2)}) collective-permute-start(bf16[64,512]{1,0:T(8,128)(2,1)S(1)} %get-tuple-element.72), channel_id=1, source_target_pairs={{0,64},{64,0},{1,65},{65,1},{2,66},{66,2},{3,67},{67,3},{4,68},{68... | collective-permute-start | bytes 196616 | tf_op jit(solution)/shard_map/ppermute | solution.py:56
  25.2 1.4 collective-permute-done.1
  26.6 8.4 %collective-permute-start.2 = (bf16[64,512]{1,0:T(8,128)(2,1)S(1)}, bf16[64,512]{1,0:T(8,128)(2,1)S(1)}, u32[]{:S(2)}, u32[]{:S(2)}) collective-permute-start(bf16[64,512]{1,0:T(8,128)(2,1)S(1)} %collective-permute-done.1), channel_id=1, source_target_pairs={{0,68},{1,69},{2,70},{3,71},{4,0},{5,1},{6,2},{7,3},{64,4},{65,5},... | collective-permute-start | bytes 196616 | tf_op jit(solution)/shard_map/ppermute | solution.py:58
  35.0 0.1 collective-permute-done
  35.1 7.9 %collective-permute-done.2 = bf16[64,512]{1,0:T(8,128)(2,1)S(1)} collective-permute-done((bf16[64,512]{1,0:T(8,128)(2,1)S(1)}, bf16[64,512]{1,0:T(8,128)(2,1)S(1)}, u32[]{:S(2)}, u32[]{:S(2)}) %collective-permute-start.2) | collective-permute-done | bytes 65568 | tf_op jit(solution)/shard_map/ppermute | solution.py:58
  43.1 1.8 maximum_select_fusion
  44.9 0.0 all-gather.2.cloned.1.call-update
  44.9 0.9 convert_element_type.66
  45.8 0.7 convert_element_type.68
  46.5 0.7 add_select_fusion.1
  47.2 0.5 fusion.15
  47.7 0.0 copy-start.1
  47.7 0.7 fusion.41
  48.4 1.7 fusion.2
  50.2 0.1 copy.26
  50.3 0.8 copy.17
  51.1 4.6 %all-to-all-start = ((f32[8,128,66]{1,2,0:T(8,128)}), f32[8,128,66]{1,2,0:T(8,128)S(1)}, u32[]{:S(2)}, u32[]{:S(2)}) async-start(f32[8,128,66]{1,2,0:T(8,128)} %copy.17), calls=%async_computation | async-start | bytes 589824 | tf_op jit(solution)/shard_map/all_to_all | solution.py:76
  55.7 0.0 copy-done
  55.7 0.7 copy.20
  56.3 0.1 copy.21
  56.4 0.0 copy-done.1
  56.5 0.2 copy.19
  56.6 17.1 %all-to-all-done = f32[8,128,66]{1,2,0:T(8,128)S(1)} async-done(((f32[8,128,66]{1,2,0:T(8,128)}), f32[8,128,66]{1,2,0:T(8,128)S(1)}, u32[]{:S(2)}, u32[]{:S(2)}) %all-to-all-start) | async-done | bytes 270368 | tf_op jit(solution)/shard_map/all_to_all | solution.py:76
  73.7 0.1 copy.31
  73.8 0.1 copy.27
  73.9 0.1 fusion.48
  74.0 0.1 fusion.46
  74.0 0.1 fusion.47
  74.1 34.4 %all-gather.2.cloned.1.call-done = bf16[4096,1024]{1,0:T(8,128)(2,1)} async-done(((bf16[128,1024]{1,0:T(8,128)(2,1)}), bf16[4096,1024]{1,0:T(8,128)(2,1)}) %all-gather.2.cloned.1.call-update) | async-done | bytes 8388624 | tf_op jit(solution)/shard_map/all_gather | solution.py:83
  108.5 9.7 %subtract_convert_fusion = bf16[128,1024]{1,0:T(8,128)(2,1)S(1)} fusion(s32[1024]{0:T(1024)S(1)} %bitcast.183, bf16[4096,1024]{1,0:T(8,128)(2,1)} %all-gather.2.cloned.1.call-done, bf16[128,4096]{0,1:T(8,128)(2,1)S(1)} %bitcast.111, bf16[128,1024]{0,1:T(8,128)(2,1)S(1)} %copy.19, f32[1024]{0:T(1024)S(1)} %bitcast.144, f32[1024]{0:T(1024)S(1)} %bitcast.145, ...), kind=kOutput, calls=%fused_computation.23 | convolution fusion | flops 1369178112 | bytes 10227712 | tf_op jit(solution)/shard_map/dot_general | solution.py:91
  118.2 0.0 copy-start.2
  118.2 1.9 %fusion.5 = bf16[128,2048]{1,0:T(8,128)(2,1)S(1)} fusion(bf16[128,1024]{1,0:T(8,128)(2,1)S(1)} %subtract_convert_fusion, s32[1024]{0:T(1024)S(1)} %bitcast.182), kind=kOutput, calls=%fused_computation.9 | convolution fusion | flops 539230208 | bytes 790528 | tf_op jit(solution)/shard_map/dot_general | solution.py:98
  120.2 38.9 %all_to_all.15 = bf16[128,8,256]{2,0,1:T(8,128)(2,1)S(1)} all-to-all(bf16[128,8,256]{2,0,1:T(8,128)(2,1)S(1)} %bitcast.107), channel_id=1, replica_groups=mesh['x'=4,'zh'=2,'y'=4,'c'=2,'trade'=8] {'trade'}, dimensions={1} | all-to-all | bytes 1048576 | tf_op jit(solution)/shard_map/all_to_all | solution.py:100
  159.1 0.1 convert_reduce_fusion
  159.2 0.0 copy-done.2
  159.2 0.3 fusion.36
  159.5 15.6 %all_to_all.16 = f32[128,8,32]{0,2,1:T(8,128)S(1)} all-to-all(f32[128,8,32]{0,2,1:T(8,128)S(1)} %bitcast.115), channel_id=1, replica_groups=mesh['x'=4,'zh'=2,'y'=4,'c'=2,'trade'=8] {'trade'}, dimensions={1} | all-to-all | bytes 262144 | tf_op jit(solution)/shard_map/all_to_all | solution.py:106
  175.1 0.6 reduce_sum.29
  (8 shorter events, 0.1 us)
Async XLA Ops:
  6.5 49.1 %copy-start = (bf16[128,4096]{1,0:T(8,128)(2,1)S(1)}, bf16[128,4096]{1,0:T(8,128)(2,1)}, u32[]{:S(2)}) copy-start(bf16[128,4096]{1,0:T(8,128)(2,1)} %param.7) | copy-start | bytes 3145732
  6.5 101.9 %all-gather.2.cloned.1.call-start = ((), (), s32[]{:S(2)}) async-start(), calls=%async_computation.3 | async-start | bytes 8650752 | tf_op jit(solution)/shard_map/all_gather | solution.py:83
  7.5 19.1 %collective-permute-start.1 = (bf16[64,512]{1,0:T(8,128)(2,1)S(1)}, bf16[64,512]{1,0:T(8,128)(2,1)S(1)}, u32[]{:S(2)}, u32[]{:S(2)}) collective-permute-start(bf16[64,512]{1,0:T(8,128)(2,1)S(1)} %get-tuple-element.71), channel_id=1, source_target_pairs={{0,68},{1,69},{2,70},{3,71},{4,0},{5,1},{6,2},{7,3},{64,4},{65,5},... | collective-permute-start | bytes 196616 | tf_op jit(solution)/shard_map/ppermute | solution.py:58
  20.3 14.9 %collective-permute-start = (bf16[64,512]{1,0:T(8,128)(2,1)S(1)}, bf16[64,512]{1,0:T(8,128)(2,1)S(1)}, u32[]{:S(2)}, u32[]{:S(2)}) collective-permute-start(bf16[64,512]{1,0:T(8,128)(2,1)S(1)} %get-tuple-element.72), channel_id=1, source_target_pairs={{0,64},{64,0},{1,65},{65,1},{2,66},{66,2},{3,67},{67,3},{4,68},{68... | collective-permute-start | bytes 196616 | tf_op jit(solution)/shard_map/ppermute | solution.py:56
  26.6 16.5 %collective-permute-start.2 = (bf16[64,512]{1,0:T(8,128)(2,1)S(1)}, bf16[64,512]{1,0:T(8,128)(2,1)S(1)}, u32[]{:S(2)}, u32[]{:S(2)}) collective-permute-start(bf16[64,512]{1,0:T(8,128)(2,1)S(1)} %collective-permute-done.1), channel_id=1, source_target_pairs={{0,68},{1,69},{2,70},{3,71},{4,0},{5,1},{6,2},{7,3},{64,4},{65,5},... | collective-permute-start | bytes 196616 | tf_op jit(solution)/shard_map/ppermute | solution.py:58
  47.7 8.8 %copy-start.1 = (bf16[128,1024]{1,0:T(8,128)(2,1)S(1)}, bf16[128,1024]{1,0:T(8,128)(2,1)}, u32[]{:S(2)}) copy-start(bf16[128,1024]{1,0:T(8,128)(2,1)} %param.9) | copy-start | bytes 786436
  51.1 22.6 %all-to-all-start = ((f32[8,128,66]{1,2,0:T(8,128)}), f32[8,128,66]{1,2,0:T(8,128)S(1)}, u32[]{:S(2)}, u32[]{:S(2)}) async-start(f32[8,128,66]{1,2,0:T(8,128)} %copy.17), calls=%async_computation | async-start | bytes 589824 | tf_op jit(solution)/shard_map/all_to_all | solution.py:76
  118.2 41.0 %copy-start.2 = (s32[256]{0:T(256)S(1)}, s32[256]{0:T(256)}, u32[]{:S(2)}) copy-start(s32[256]{0:T(256)} %param.13) | copy-start | bytes 3076
Sparse Core Ops, SparseCore 0:
  45.0 63.4 all-gather.1

commit v9 on v4

--- a/solution.py
+++ b/solution.py
@@ -4,6 +4,7 @@
 from jax.sharding import Mesh, PartitionSpec as P
 
 CP_DEV = 32
+ROOM = 304
 
 
 def clenshaw(chosen, coeffs_t):
@@ -60,8 +61,12 @@
         [coeffs.astype(jnp.float32), offset[:, None], trade_ns.astype(jnp.float32)[:, None]], axis=1
     )
     sent = jnp.dot(place.T, table, precision=lax.Precision.HIGHEST)
-    got = lax.all_to_all(sent.reshape(owners, per, terms + 2), "trade", 0, 0, tiled=False)
-    got = got.reshape(count, terms + 2)
+    sets = ns_cp.shape[0]
+    spread = jnp.broadcast_to(ns_cp.astype(jnp.float32).reshape(sets // per, per).T, (owners, per, sets // per))
+    sent = jnp.concatenate([sent.reshape(owners, per, terms + 2), spread], axis=2)
+    got = lax.all_to_all(sent, "trade", 0, 0, tiled=False)
+    all_cp = got[:, :, terms + 2 :].transpose(0, 2, 1).reshape(owners * sets).astype(jnp.int32)
+    got = got[:, :, : terms + 2].reshape(count, terms + 2)
     got_coeffs = got[:, :terms].astype(jnp.bfloat16)
     got_col = got[:, terms].astype(jnp.int32)
     got_ns = got[:, terms + 1].astype(jnp.int32)
@@ -78,19 +83,57 @@
     chosen = jnp.dot(factors, pick, preferred_element_type=jnp.float32).astype(jnp.bfloat16)
     values = clenshaw(chosen, got_coeffs.astype(jnp.float32).T)
 
-    total_sets = ns_cp.shape[0] * owners
-    net_table = (got_ns[:, None] == jnp.arange(total_sets, dtype=jnp.int32)[None, :]).astype(
-        jnp.bfloat16
-    )
-    netting = jnp.dot(values, net_table, preferred_element_type=jnp.float32)
-    shares = jnp.sum(lax.all_to_all(netting.reshape(rows, owners, -1), "trade", 1, 1, tiled=False), axis=1)
-    positive = jnp.maximum(shares, 0.0).astype(jnp.bfloat16)
-    cp_table = (ns_cp[:, None] == jnp.arange(CP_DEV * owners, dtype=jnp.int32)[None, :]).astype(
-        jnp.bfloat16
-    )
-    partial_cp = jnp.dot(positive, cp_table, preferred_element_type=jnp.float32)
-    pieces = lax.all_to_all(partial_cp.reshape(rows, owners, CP_DEV), "trade", 1, 1, tiled=False)
-    return jnp.sum(pieces, axis=1).T
+    def by_set_owner(values):
+        total_sets = sets * owners
+        net_table = (got_ns[:, None] == jnp.arange(total_sets, dtype=jnp.int32)[None, :]).astype(
+            jnp.bfloat16
+        )
+        netting = jnp.dot(values, net_table, preferred_element_type=jnp.float32)
+        sent = netting.astype(jnp.bfloat16).reshape(rows, owners, -1)
+        shares = jnp.sum(lax.all_to_all(sent, "trade", 1, 1, tiled=False).astype(jnp.float32), axis=1)
+        positive = jnp.maximum(shares, 0.0).astype(jnp.bfloat16)
+        cp_table = (ns_cp[:, None] == jnp.arange(CP_DEV * owners, dtype=jnp.int32)[None, :]).astype(
+            jnp.bfloat16
+        )
+        partial_cp = jnp.dot(positive, cp_table, preferred_element_type=jnp.float32)
+        pieces = lax.all_to_all(partial_cp.reshape(rows, owners, CP_DEV), "trade", 1, 1, tiled=False)
+        return jnp.sum(pieces, axis=1).T
+
+    total_sets = sets * owners
+    boss = all_cp // CP_DEV
+    mask = (boss[:, None] == jnp.arange(owners, dtype=jnp.int32)[None, :]).astype(jnp.bfloat16)
+    lower = (
+        jnp.arange(total_sets, dtype=jnp.int32)[:, None] >= jnp.arange(total_sets, dtype=jnp.int32)[None, :]
+    ).astype(jnp.bfloat16)
+    running = jnp.dot(lower, mask, preferred_element_type=jnp.float32)
+    rank = jnp.sum(running * mask.astype(jnp.float32), axis=1).astype(jnp.int32) - 1
+    fits = jnp.max(rank) < ROOM
+    slot = boss * ROOM + rank
+
+    def by_cp_owner(values):
+        trade_slot = jnp.take(slot, got_ns)
+        route = (trade_slot[None, :] == jnp.arange(owners * ROOM, dtype=jnp.int32)[:, None]).astype(
+            jnp.bfloat16
+        )
+        routed = lax.dot_general(
+            route, values, (((1,), (1,)), ((), ())), preferred_element_type=jnp.float32
+        )
+        sent = routed.astype(jnp.bfloat16).reshape(owners, ROOM, rows)
+        netting = jnp.sum(lax.all_to_all(sent, "trade", 0, 0, tiled=False).astype(jnp.float32), axis=0)
+        positive = jnp.maximum(netting, 0.0).astype(jnp.bfloat16)
+        here = lax.axis_index("trade")
+        at_slot = (
+            (boss[:, None] == here) & (rank[:, None] == jnp.arange(ROOM, dtype=jnp.int32)[None, :])
+        ).astype(jnp.bfloat16)
+        of_cp = (
+            all_cp[:, None] == here * CP_DEV + jnp.arange(CP_DEV, dtype=jnp.int32)[None, :]
+        ).astype(jnp.bfloat16)
+        cp_table = lax.dot_general(
+            of_cp, at_slot, (((0,), (0,)), ((), ())), preferred_element_type=jnp.float32
+        ).astype(jnp.bfloat16)
+        return jnp.dot(cp_table, positive, preferred_element_type=jnp.float32)
+
+    return lax.cond(fits, by_cp_owner, by_set_owner, values)
 
 
 PATH = ("x", "zh", "y", "c")

time: 198 us -> 172 us (0.87)
  blocking collectives: 97.2 us -> 20.2 us
  waiting for transfers between devices: 53.9 us -> 84.4 us
  starting transfers between devices: 13.6 us -> 23.5 us
  local copies, waits for them, and re-layouts: 2.06 us -> 8.01 us
  matrix products: 13.1 us -> 16.5 us
    all_to_all x2 -> x0, blocking collectives: 77 us -> none  [the longest x1 61.4 us: per_device(): lax.all_to_all(netting.reshape(rows, owners, -1), 'trade', 1, 1, tiled=Fa...]
    all_to_all x1 -> x2, waiting for transfers between devices: 17.1 us -> 50.4 us  [the longest x1 33.3 us: by_cp_owner(): lax.all_to_all(sent, 'trade', 0, 0, tiled=False).astype(jnp.float32)]
    all_to_all x1 -> x2, starting transfers between devices: 13.6 us -> 23.5 us  [the longest x1 13.6 us: per_device(): got = lax.all_to_all(sent, 'trade', 0, 0, tiled=False)]
    gather x0 -> x1, local copies, waits for them, and re-layouts: none -> 6.15 us  [by_cp_owner(): trade_slot = jnp.take(slot, got_ns)]
    dot_general x2 -> x3, matrix products: 2.21 us -> 5.6 us  [the longest x1 2.63 us: by_cp_owner(): lax.dot_general(route, values, (((1,), (1,)), ((), ())), preferred_elemen...]
    all_gather x1, waiting for transfers between devices: 36.7 us -> 33.9 us  [per_device(): gathered = lax.all_gather(gathered, ('x', 'y', 'c'), axis=0, tiled=True)]
  transfers between devices with their start and end apart: 2 -> 3, of which waited for: 2 -> 3; matrix products, arithmetic and copies ran while one was open for 4% -> 5% of each run, Pallas kernels for 0% -> 0%
where the time goes in v9:
time: 172 us
  waiting for transfers between devices  84.4 us (49%)
  starting transfers between devices  23.5 us (14%)
  blocking collectives  20.2 us (12%)
  matrix products  16.5 us (10%)
  between operations  14.2 us (8%)
  local copies, waits for them, and re-layouts  8.01 us (5%)
  other arithmetic  4.58 us (3%)
    all_gather x1, waiting for transfers between devices, per_device(): gathered = lax.all_gather(gathered, ('x', 'y', 'c'), axis=0, tiled=True)  33.9 us
    all_to_all x1, waiting for transfers between devices, by_cp_owner(): lax.all_to_all(sent, 'trade', 0, 0, tiled=False).astype(jnp.float32)  33.3 us
    all_gather x1, blocking collectives, per_device(): gathered = lax.all_gather(loadings, 'zh', axis=0, tiled=True)  20.2 us
    all_to_all x1, waiting for transfers between devices, per_device(): got = lax.all_to_all(sent, 'trade', 0, 0, tiled=False)  17.1 us
    all_to_all x1, starting transfers between devices, per_device(): got = lax.all_to_all(sent, 'trade', 0, 0, tiled=False)  13.6 us
    all_to_all x1, starting transfers between devices, by_cp_owner(): lax.all_to_all(sent, 'trade', 0, 0, tiled=False).astype(jnp.float32)  9.98 us
    dot_general x1, matrix products, per_device(): jnp.dot(factors, pick, preferred_element_type=jnp.float32)  8.71 us
    gather x1, local copies, waits for them, and re-layouts, by_cp_owner(): trade_slot = jnp.take(slot, got_ns)  6.15 us
  transfers between devices with their start and end apart: 3, of which 3 were waited for; matrix products, arithmetic and copies ran while one was open for 5% of the time, Pallas kernels for 0%

profile of v9, /device:TPU:6, one launch (start us, length us, event | category | flops | bytes accessed | tf_op | source)
XLA Modules:
  0.0 172.0 jit_solution(5545979340069448943)
XLA Ops:
  6.5 0.0 copy-start.2
  6.5 0.0 copy-start
  6.5 0.0 all-gather.2.cloned.1.call-start
  6.5 20.2 %all_gather.6 = bf16[128,1024]{1,0:T(8,128)(2,1)} all-gather(bf16[64,1024]{1,0:T(8,128)(2,1)} %param.10), channel_id=1, replica_groups=mesh['x'=4,'zh'=2,'y'=4,'c'=2,'trade'=8] {'zh'}, dimensions={0}, use_global_device_ids=true | all-gather | bytes 393216 | tf_op jit(solution)/shard_map/all_gather | solution.py:74
  26.8 0.0 all-gather.2.cloned.1.call-update
  26.8 0.7 convert_element_type.117
  27.5 0.9 convert_element_type.115
  28.4 0.7 add_select_fusion.2
  29.1 0.5 fusion.48
  29.6 0.7 fusion.75
  30.3 1.7 %fusion.35 = f32[1024,66]{0,1:T(8,128)S(1)} fusion(s32[1024]{0:T(1024)S(1)} %get-tuple-element.108, f32[1024,1]{0,1:T(1,128)S(1)} %bitcast.185, f32[1024,1]{0,1:T(1,128)S(1)} %bitcast.187, f32[1024,64]{0,1:T(8,128)S(1)} %convert_element_type.115), kind=kOutput, calls=%fused_computation.42 | convolution fusion | flops 831655936 | bytes 544768 | tf_op jit(solution)/shard_map/dot_general | solution.py:63
  32.1 0.1 copy.24
  32.1 0.1 copy.19
  32.2 0.0 copy-done.2
  32.2 0.8 pad_maximum_fusion
  33.0 13.6 %all-to-all-start.3 = ((f32[8,128,68]{1,2,0:T(8,128)}), f32[8,128,68]{1,2,0:T(8,128)S(1)}, u32[]{:S(2)}, u32[]{:S(2)}) async-start(f32[8,128,68]{1,2,0:T(8,128)} %pad_maximum_fusion), calls=%async_computation.3 | async-start | bytes 589824 | tf_op jit(solution)/shard_map/all_to_all | solution.py:67
  46.6 0.0 copy-done
  46.6 0.7 copy.21
  47.3 0.1 copy.22
  47.4 0.0 copy-start.3
  47.4 17.1 %all-to-all-done.3 = f32[8,128,68]{1,2,0:T(8,128)S(1)} async-done(((f32[8,128,68]{1,2,0:T(8,128)}), f32[8,128,68]{1,2,0:T(8,128)S(1)}, u32[]{:S(2)}, u32[]{:S(2)}) %all-to-all-start.3) | async-done | bytes 278560 | tf_op jit(solution)/shard_map/all_to_all | solution.py:67
  64.5 1.4 fusion.46
  65.9 0.6 convert_add_fusion
  67.2 0.1 copy.27
  67.3 0.1 copy.25
  67.5 0.1 fusion.80
  67.5 0.1 fusion.81
  67.6 0.1 fusion.82
  67.7 33.9 %all-gather.2.cloned.1.call-done = bf16[4096,1024]{1,0:T(8,128)(2,1)} async-done(((bf16[128,1024]{1,0:T(8,128)(2,1)}), bf16[4096,1024]{1,0:T(8,128)(2,1)}) %all-gather.2.cloned.1.call-update) | async-done | bytes 8388624 | tf_op jit(solution)/shard_map/all_gather | solution.py:75
  101.6 0.0 copy-done.3
  101.6 8.7 %subtract_convert_fusion = bf16[128,1024]{1,0:T(8,128)(2,1)S(1)} fusion(s32[1024]{0:T(1024)S(1)} %bitcast.186, bf16[128,4096]{0,1:T(8,128)(2,1)S(1)} %bitcast.110, bf16[4096,1024]{1,0:T(8,128)(2,1)} %all-gather.2.cloned.1.call-done, bf16[128,1024]{1,0:T(8,128)(2,1)S(1)} %copy-done.3, f32[1024]{0:T(1024)S(1)} %bitcast.129, f32[1024]{0:T(1024)S(1)} %bitcast.130, ...), kind=kOutput, calls=%fused_computation.57 | convolution fusion | flops 1369178112 | bytes 10227712 | tf_op jit(solution)/shard_map/dot_general | solution.py:83
  110.3 54.2 %conditional.1 = (f32[32,128]{1,0:T(8,128)S(1)}) conditional(s32[]{:T(128)} %convert_element_type.125, (s32[1024]{0:T(1024)S(1)}, bf16[128,1024]{1,0:T(8,128)(2,1)S(1)}, s32[256]{0:T(256)S(1)}) %tuple.86, (s32[2048]{0:T(1024)S(1)}, s32[2048]{0:T(1024)S(1)}, s32[2048]{0:T(1024)S(1)}, s32[1024]{0:T(1024)S(1)}, bf16[128,1024]{1,0:T(8,128)(2,1)S(1)}) %tuple.84), branch_computations={%region_3.6_spmd, %region_6.8_spmd} | conditional | flops 684710464 | bytes 3637584 | solution.py:136
  110.6 6.2 %gather_fusion = s32[1024]{0:T(1024)S(1)} fusion(s32[2048]{0:T(1024)S(1)} %multiply_add_fusion, s32[1024]{0:T(1024)S(1)} %fusion.32), kind=kCustom, calls=%fused_computation | custom fusion | bytes 12288 | tf_op jit(solution)/shard_map/cond/branch_1_fun/jit(_take)/gather | solution.py:114
  116.7 2.6 %fusion.13 = bf16[2432,128]{1,0:T(8,128)(2,1)} fusion(bf16[128,1024]{1,0:T(8,128)(2,1)S(1)} %get-tuple-element.37, s32[1024]{0:T(1024)S(1)} %and_select_fusion), kind=kOutput, calls=%fused_computation.16 | convolution fusion | flops 640335872 | bytes 888832 | tf_op jit(solution)/shard_map/cond/branch_1_fun/dot_general | solution.py:118
  119.4 10.0 %all-to-all-start.2 = ((bf16[8,304,128]{2,1,0:T(8,128)(2,1)}), bf16[8,304,128]{2,1,0:T(8,128)(2,1)S(1)}, u32[]{:S(2)}, u32[]{:S(2)}) async-start(bf16[8,304,128]{2,1,0:T(8,128)(2,1)} %bitcast.4), calls=%async_computation.2 | async-start | bytes 1245184 | tf_op jit(solution)/shard_map/cond/branch_1_fun/all_to_all | solution.py:122
  129.4 33.3 %all-to-all-done.2 = bf16[8,304,128]{2,1,0:T(8,128)(2,1)S(1)} async-done(((bf16[8,304,128]{2,1,0:T(8,128)(2,1)}), bf16[8,304,128]{2,1,0:T(8,128)(2,1)S(1)}, u32[]{:S(2)}, u32[]{:S(2)}) %all-to-all-start.2) | async-done | bytes 622624 | tf_op jit(solution)/shard_map/cond/branch_1_fun/all_to_all | solution.py:122
  162.7 0.1 convert_reduce_fusion.1
  162.8 1.5 fusion.23
  164.5 0.0 copy-start.1
  164.5 0.6 copy-done.1
  (14 shorter events, 0.1 us)
Async XLA Ops:
  6.5 25.7 %copy-start.2 = (s32[256]{0:T(256)S(1)}, s32[256]{0:T(256)}, u32[]{:S(2)}) copy-start(s32[256]{0:T(256)} %param.15) | copy-start | bytes 3076
  6.5 40.0 %copy-start = (bf16[128,4096]{1,0:T(8,128)(2,1)S(1)}, bf16[128,4096]{1,0:T(8,128)(2,1)}, u32[]{:S(2)}) copy-start(bf16[128,4096]{1,0:T(8,128)(2,1)} %param.9) | copy-start | bytes 3145732
  6.5 95.1 %all-gather.2.cloned.1.call-start = ((), (), s32[]{:S(2)}) async-start(), calls=%async_computation.4 | async-start | bytes 8650752 | tf_op jit(solution)/shard_map/all_gather | solution.py:75
  33.0 31.5 %all-to-all-start.3 = ((f32[8,128,68]{1,2,0:T(8,128)}), f32[8,128,68]{1,2,0:T(8,128)S(1)}, u32[]{:S(2)}, u32[]{:S(2)}) async-start(f32[8,128,68]{1,2,0:T(8,128)} %pad_maximum_fusion), calls=%async_computation.3 | async-start | bytes 589824 | tf_op jit(solution)/shard_map/all_to_all | solution.py:67
  47.4 54.2 %copy-start.3 = (bf16[128,1024]{1,0:T(8,128)(2,1)S(1)}, bf16[128,1024]{1,0:T(8,128)(2,1)}, u32[]{:S(2)}) copy-start(bf16[128,1024]{1,0:T(8,128)(2,1)} %param.11) | copy-start | bytes 786436
  119.4 43.3 %all-to-all-start.2 = ((bf16[8,304,128]{2,1,0:T(8,128)(2,1)}), bf16[8,304,128]{2,1,0:T(8,128)(2,1)S(1)}, u32[]{:S(2)}, u32[]{:S(2)}) async-start(bf16[8,304,128]{2,1,0:T(8,128)(2,1)} %bitcast.4), calls=%async_computation.2 | async-start | bytes 1245184 | tf_op jit(solution)/shard_map/cond/branch_1_fun/all_to_all | solution.py:122
  164.5 0.6 copy-start.1
Sparse Core Ops, SparseCore 0:
  26.9 74.6 all-gather.1

commit v10 on v9

--- a/solution.py
+++ b/solution.py
@@ -110,8 +110,21 @@
     fits = jnp.max(rank) < ROOM
     slot = boss * ROOM + rank
 
+    trade_slot = jnp.take(slot, got_ns)
+    here = lax.axis_index("trade")
+    at_slot = (
+        (boss[:, None] == here) & (rank[:, None] == jnp.arange(ROOM, dtype=jnp.int32)[None, :])
+    ).astype(jnp.bfloat16)
+    of_cp = (all_cp[:, None] == here * CP_DEV + jnp.arange(CP_DEV, dtype=jnp.int32)[None, :]).astype(
+        jnp.bfloat16
+    )
+    cp_table = lax.dot_general(
+        of_cp, at_slot, (((0,), (0,)), ((), ())), preferred_element_type=jnp.float32
+    ).astype(jnp.bfloat16)
+
+    trade_slot, cp_table = lax.optimization_barrier((trade_slot, cp_table))
+
     def by_cp_owner(values):
-        trade_slot = jnp.take(slot, got_ns)
         route = (trade_slot[None, :] == jnp.arange(owners * ROOM, dtype=jnp.int32)[:, None]).astype(
             jnp.bfloat16
         )
@@ -121,16 +134,6 @@
         sent = routed.astype(jnp.bfloat16).reshape(owners, ROOM, rows)
         netting = jnp.sum(lax.all_to_all(sent, "trade", 0, 0, tiled=False).astype(jnp.float32), axis=0)
         positive = jnp.maximum(netting, 0.0).astype(jnp.bfloat16)
-        here = lax.axis_index("trade")
-        at_slot = (
-            (boss[:, None] == here) & (rank[:, None] == jnp.arange(ROOM, dtype=jnp.int32)[None, :])
-        ).astype(jnp.bfloat16)
-        of_cp = (
-            all_cp[:, None] == here * CP_DEV + jnp.arange(CP_DEV, dtype=jnp.int32)[None, :]
-        ).astype(jnp.bfloat16)
-        cp_table = lax.dot_general(
-            of_cp, at_slot, (((0,), (0,)), ((), ())), preferred_element_type=jnp.float32
-        ).astype(jnp.bfloat16)
         return jnp.dot(cp_table, positive, preferred_element_type=jnp.float32)
 
     return lax.cond(fits, by_cp_owner, by_set_owner, values)

time: 172 us -> 163 us (0.948)
  blocking collectives: 20.2 us -> 63.4 us
  waiting for transfers between devices: 84.4 us -> 43.4 us
  starting transfers between devices: 23.5 us -> 13.6 us
    all_to_all x0 -> x1, blocking collectives: none -> 43.1 us  [by_cp_owner(): lax.all_to_all(sent, 'trade', 0, 0, tiled=False).astype(jnp.float32)]
    all_to_all x1 -> x0, waiting for transfers between devices: 33.3 us -> none  [by_cp_owner(): lax.all_to_all(sent, 'trade', 0, 0, tiled=False).astype(jnp.float32)]
    all_to_all x1 -> x0, starting transfers between devices: 9.98 us -> none  [by_cp_owner(): lax.all_to_all(sent, 'trade', 0, 0, tiled=False).astype(jnp.float32)]
    all_gather x1, waiting for transfers between devices: 33.9 us -> 26.3 us  [per_device(): gathered = lax.all_gather(gathered, ('x', 'y', 'c'), axis=0, tiled=True)]
  transfers between devices with their start and end apart: 3 -> 2, of which waited for: 3 -> 2; matrix products, arithmetic and copies ran while one was open for 5% -> 10% of each run, Pallas kernels for 0% -> 0%
where the time goes in v10:
time: 163 us
  blocking collectives  63.4 us (39%)
  waiting for transfers between devices  43.4 us (27%)
  matrix products  15.7 us (10%)
  between operations  14.3 us (9%)
  starting transfers between devices  13.6 us (8%)
  local copies, waits for them, and re-layouts  7.99 us (5%)
  other arithmetic  4.59 us (3%)
    all_to_all x1, blocking collectives, by_cp_owner(): lax.all_to_all(sent, 'trade', 0, 0, tiled=False).astype(jnp.float32)  43.1 us
    all_gather x1, waiting for transfers between devices, per_device(): gathered = lax.all_gather(gathered, ('x', 'y', 'c'), axis=0, tiled=True)  26.3 us
    all_gather x1, blocking collectives, per_device(): gathered = lax.all_gather(loadings, 'zh', axis=0, tiled=True)  20.3 us
    all_to_all x1, waiting for transfers between devices, per_device(): got = lax.all_to_all(sent, 'trade', 0, 0, tiled=False)  17.1 us
    all_to_all x1, starting transfers between devices, per_device(): got = lax.all_to_all(sent, 'trade', 0, 0, tiled=False)  13.6 us
    dot_general x1, matrix products, per_device(): jnp.dot(factors, pick, preferred_element_type=jnp.float32)  8.73 us
    gather x1, local copies, waits for them, and re-layouts, per_device(): trade_slot = jnp.take(slot, got_ns)  6.15 us
  transfers between devices with their start and end apart: 2, of which 2 were waited for; matrix products, arithmetic and copies ran while one was open for 10% of the time, Pallas kernels for 0%

profile of v10, /device:TPU:6, one launch (start us, length us, event | category | flops | bytes accessed | tf_op | source)
XLA Modules:
  0.0 163.0 jit_solution(16010894407590008009)
XLA Ops:
  6.5 0.0 copy-start.2
  6.5 0.0 copy-start
  6.5 0.0 all-gather.2.cloned.1.call-start
  6.5 20.3 %all_gather.6 = bf16[128,1024]{1,0:T(8,128)(2,1)} all-gather(bf16[64,1024]{1,0:T(8,128)(2,1)} %param.10), channel_id=1, replica_groups=mesh['x'=4,'zh'=2,'y'=4,'c'=2,'trade'=8] {'zh'}, dimensions={0}, use_global_device_ids=true | all-gather | bytes 393216 | tf_op jit(solution)/shard_map/all_gather | solution.py:74
  26.8 0.0 all-gather.2.cloned.1.call-update
  26.8 0.7 convert_element_type.132
  27.5 0.9 convert_element_type.130
  28.4 0.7 add_select_fusion.2
  29.1 0.5 fusion.38
  29.6 0.7 fusion.68
  30.3 1.7 %fusion.17 = f32[1024,66]{0,1:T(8,128)S(1)} fusion(s32[1024]{0:T(1024)S(1)} %get-tuple-element.109, f32[1024,1]{0,1:T(1,128)S(1)} %bitcast.190, f32[1024,1]{0,1:T(1,128)S(1)} %bitcast.193, f32[1024,64]{0,1:T(8,128)S(1)} %convert_element_type.130), kind=kOutput, calls=%fused_computation.27 | convolution fusion | flops 831655936 | bytes 544768 | tf_op jit(solution)/shard_map/dot_general | solution.py:63
  32.1 0.1 copy.25
  32.2 0.1 copy.20
  32.2 0.0 copy-done.2
  32.3 0.8 pad_maximum_fusion
  33.0 13.6 %all-to-all-start.3 = ((f32[8,128,68]{1,2,0:T(8,128)}), f32[8,128,68]{1,2,0:T(8,128)S(1)}, u32[]{:S(2)}, u32[]{:S(2)}) async-start(f32[8,128,68]{1,2,0:T(8,128)} %pad_maximum_fusion), calls=%async_computation.3 | async-start | bytes 589824 | tf_op jit(solution)/shard_map/all_to_all | solution.py:67
  46.6 0.0 copy-done
  46.6 0.7 copy.22
  47.2 0.1 copy.23
  47.3 17.1 %all-to-all-done.3 = f32[8,128,68]{1,2,0:T(8,128)S(1)} async-done(((f32[8,128,68]{1,2,0:T(8,128)}), f32[8,128,68]{1,2,0:T(8,128)S(1)}, u32[]{:S(2)}, u32[]{:S(2)}) %all-to-all-start.3) | async-done | bytes 278560 | tf_op jit(solution)/shard_map/all_to_all | solution.py:67
  64.5 1.4 fusion.33
  65.9 0.6 convert_add_fusion
  67.2 0.1 copy.28
  67.3 0.0 copy-start.3
  67.3 0.1 copy.26
  67.4 6.2 %gather_fusion = s32[1024]{0:T(1024)S(1)} fusion(s32[2048]{0:T(1024)S(1)} %get-tuple-element.107, s32[1024]{0:T(1024)S(1)} %broadcast_clamp_fusion), kind=kCustom, calls=%fused_computation | custom fusion | bytes 12288 | tf_op jit(solution)/shard_map/jit(_take)/gather | solution.py:113
  73.6 1.4 fusion.34
  75.1 0.1 fusion.73
  75.2 0.1 fusion.74
  75.3 0.1 fusion.75
  75.3 26.3 %all-gather.2.cloned.1.call-done = bf16[4096,1024]{1,0:T(8,128)(2,1)} async-done(((bf16[128,1024]{1,0:T(8,128)(2,1)}), bf16[4096,1024]{1,0:T(8,128)(2,1)}) %all-gather.2.cloned.1.call-update) | async-done | bytes 8388624 | tf_op jit(solution)/shard_map/all_gather | solution.py:75
  101.6 0.0 copy-done.3
  101.6 8.7 %subtract_convert_fusion = bf16[128,1024]{1,0:T(8,128)(2,1)S(1)} fusion(s32[1024]{0:T(1024)S(1)} %bitcast.192, bf16[128,4096]{0,1:T(8,128)(2,1)S(1)} %bitcast.114, bf16[4096,1024]{1,0:T(8,128)(2,1)} %all-gather.2.cloned.1.call-done, bf16[128,1024]{1,0:T(8,128)(2,1)S(1)} %copy-done.3, f32[1024]{0:T(1024)S(1)} %bitcast.134, f32[1024]{0:T(1024)S(1)} %bitcast.135, ...), kind=kOutput, calls=%fused_computation.50 | convolution fusion | flops 1369178112 | bytes 10227712 | tf_op jit(solution)/shard_map/dot_general | solution.py:83
  110.3 45.2 %conditional.1 = (f32[32,128]{1,0:T(8,128)S(1)}) conditional(s32[]{:T(128)} %convert_element_type.140, (f32[1024,1]{0,1:T(1,128)S(1)}, bf16[128,1024]{1,0:T(8,128)(2,1)S(1)}, s32[256]{0:T(256)S(1)}) %tuple.90, (s32[1024]{0:T(1024)S(1)}, bf16[128,1024]{1,0:T(8,128)(2,1)S(1)}, bf16[32,304]{1,0:T(8,128)(2,1)S(1)}) %tuple.14), branch_computations={%region_3.6_spmd, %region_6.8_spmd} | conditional | flops 643526656 | bytes 3044364 | solution.py:139
  110.4 1.8 %fusion.13 = bf16[2432,128]{1,0:T(8,128)(2,1)S(1)} fusion(bf16[128,1024]{1,0:T(8,128)(2,1)S(1)} %get-tuple-element.26, s32[1024]{0:T(1024)S(1)} %get-tuple-element.25), kind=kOutput, calls=%fused_computation.16 | convolution fusion | flops 640335872 | bytes 888832 | tf_op jit(solution)/shard_map/cond/branch_1_fun/dot_general | solution.py:131
  112.2 43.1 %all_to_all.19 = bf16[8,304,128]{2,1,0:T(8,128)(2,1)S(1)} all-to-all(bf16[8,304,128]{2,1,0:T(8,128)(2,1)S(1)} %bitcast.118), channel_id=1, replica_groups=mesh['x'=4,'zh'=2,'y'=4,'c'=2,'trade'=8] {'trade'}, dimensions={0} | all-to-all | bytes 1245184 | tf_op jit(solution)/shard_map/cond/branch_1_fun/all_to_all | solution.py:135
  155.3 0.1 convert_reduce_fusion.1
  155.4 0.1 convolution_bitcast_fusion
  155.5 0.0 copy-start.1
  155.5 0.6 copy-done.1
  (13 shorter events, 0.2 us)
Async XLA Ops:
  6.5 25.7 %copy-start.2 = (s32[256]{0:T(256)S(1)}, s32[256]{0:T(256)}, u32[]{:S(2)}) copy-start(s32[256]{0:T(256)} %param.15) | copy-start | bytes 3076
  6.5 40.0 %copy-start = (bf16[128,4096]{1,0:T(8,128)(2,1)S(1)}, bf16[128,4096]{1,0:T(8,128)(2,1)}, u32[]{:S(2)}) copy-start(bf16[128,4096]{1,0:T(8,128)(2,1)} %param.9) | copy-start | bytes 3145732
  6.5 95.1 %all-gather.2.cloned.1.call-start = ((), (), s32[]{:S(2)}) async-start(), calls=%async_computation.4 | async-start | bytes 8650752 | tf_op jit(solution)/shard_map/all_gather | solution.py:75
  33.0 31.5 %all-to-all-start.3 = ((f32[8,128,68]{1,2,0:T(8,128)}), f32[8,128,68]{1,2,0:T(8,128)S(1)}, u32[]{:S(2)}, u32[]{:S(2)}) async-start(f32[8,128,68]{1,2,0:T(8,128)} %pad_maximum_fusion), calls=%async_computation.3 | async-start | bytes 589824 | tf_op jit(solution)/shard_map/all_to_all | solution.py:67
  67.3 34.3 %copy-start.3 = (bf16[128,1024]{1,0:T(8,128)(2,1)S(1)}, bf16[128,1024]{1,0:T(8,128)(2,1)}, u32[]{:S(2)}) copy-start(bf16[128,1024]{1,0:T(8,128)(2,1)} %param.11) | copy-start | bytes 786436
  155.5 0.6 copy-start.1
Sparse Core Ops, SparseCore 0:
  26.9 74.6 all-gather.1

commit v11 on v10

--- a/solution.py
+++ b/solution.py
@@ -71,7 +71,9 @@
     got_col = got[:, terms].astype(jnp.int32)
     got_ns = got[:, terms + 1].astype(jnp.int32)
 
-    gathered = lax.all_gather(loadings, "zh", axis=0, tiled=True)
+    partner = lax.ppermute(loadings, "zh", [(0, 1), (1, 0)])
+    first = lax.axis_index("zh") == 0
+    gathered = jnp.where(first, jnp.concatenate([loadings, partner]), jnp.concatenate([partner, loadings]))
     gathered = lax.all_gather(gathered, ("x", "y", "c"), axis=0, tiled=True)
     rows = drivers.shape[0]
     lead = loadings.shape[0]

time: 163 us -> 168 us (1.031)
  blocking collectives: 63.4 us -> 43.1 us
  starting transfers between devices: 13.6 us -> 31.1 us
  waiting for transfers between devices: 43.4 us -> 47.6 us
  other arithmetic: 4.59 us -> 6.36 us
    all_gather x1 -> x0, blocking collectives: 20.3 us -> none  [per_device(): gathered = lax.all_gather(loadings, 'zh', axis=0, tiled=True)]
    ppermute x0 -> x1, starting transfers between devices: none -> 15.8 us  [per_device(): partner = lax.ppermute(loadings, 'zh', [(0, 1), (1, 0)])]
    ppermute x0 -> x1, waiting for transfers between devices: none -> 3.99 us  [per_device(): partner = lax.ppermute(loadings, 'zh', [(0, 1), (1, 0)])]
    select_n x0 -> x1, other arithmetic: none -> 1.76 us  [per_device(): jnp.where(first, jnp.concatenate([loadings, partner]), jnp.concatenate([p...]
  transfers between devices with their start and end apart: 2 -> 3, of which waited for: 2 -> 3; matrix products, arithmetic and copies ran while one was open for 10% -> 10% of each run, Pallas kernels for 0% -> 0%
where the time goes in v11:
time: 168 us; the launch traced here: 167 us
  waiting for transfers between devices  47.6 us (28%)
  blocking collectives  43.1 us (26%)
  starting transfers between devices  31.1 us (19%)
  matrix products  16.8 us (10%)
  between operations  14.3 us (9%)
  local copies, waits for them, and re-layouts  8.15 us (5%)
  other arithmetic  6.36 us (4%)
    all_to_all x1, blocking collectives, by_cp_owner(): lax.all_to_all(sent, 'trade', 0, 0, tiled=False).astype(jnp.float32)  43.1 us
    all_gather x1, waiting for transfers between devices, per_device(): gathered = lax.all_gather(gathered, ('x', 'y', 'c'), axis=0, tiled=True)  26.7 us
    all_to_all x1, waiting for transfers between devices, per_device(): got = lax.all_to_all(sent, 'trade', 0, 0, tiled=False)  16.9 us
    ppermute x1, starting transfers between devices, per_device(): partner = lax.ppermute(loadings, 'zh', [(0, 1), (1, 0)])  15.8 us
    all_to_all x1, starting transfers between devices, per_device(): got = lax.all_to_all(sent, 'trade', 0, 0, tiled=False)  15.2 us
    dot_general x1, matrix products, per_device(): jnp.dot(factors, pick, preferred_element_type=jnp.float32)  9.77 us
    gather x1, local copies, waits for them, and re-layouts, per_device(): trade_slot = jnp.take(slot, got_ns)  6.15 us
    ppermute x1, waiting for transfers between devices, per_device(): partner = lax.ppermute(loadings, 'zh', [(0, 1), (1, 0)])  3.99 us
  transfers between devices with their start and end apart: 3, of which 3 were waited for; matrix products, arithmetic and copies ran while one was open for 10% of the time, Pallas kernels for 0%

profile of v11, /device:TPU:6, one launch (start us, length us, event | category | flops | bytes accessed | tf_op | source)
XLA Modules:
  0.0 167.4 jit_solution(676193153237594487)
XLA Ops:
  6.5 0.0 copy-start.3
  6.5 0.0 copy-start
  6.5 0.0 all-gather.2.cloned.1.call-start
  6.5 15.8 %collective-permute-start = (bf16[64,1024]{1,0:T(8,128)(2,1)}, bf16[64,1024]{1,0:T(8,128)(2,1)S(1)}, u32[]{:S(2)}, u32[]{:S(2)}) collective-permute-start(bf16[64,1024]{1,0:T(8,128)(2,1)} %param.10), channel_id=1, source_target_pairs={{0,64},{64,0},{1,65},{65,1},{2,66},{66,2},{3,67},{67,3},{4,68},{68... | collective-permute-start | bytes 393224 | tf_op jit(solution)/shard_map/ppermute | solution.py:74
  22.4 4.0 %collective-permute-done = bf16[64,1024]{1,0:T(8,128)(2,1)S(1)} collective-permute-done((bf16[64,1024]{1,0:T(8,128)(2,1)}, bf16[64,1024]{1,0:T(8,128)(2,1)S(1)}, u32[]{:S(2)}, u32[]{:S(2)}) %collective-permute-start) | collective-permute-done | bytes 131104 | tf_op jit(solution)/shard_map/ppermute | solution.py:74
  26.4 1.8 %maximum_select_fusion = bf16[128,1024]{1,0:T(8,128)(2,1)} fusion(bf16[64,1024]{1,0:T(8,128)(2,1)S(1)} %collective-permute-done, bf16[64,1024]{1,0:T(8,128)(2,1)} %param.10, pred[]{:T(512)S(6)} %eq.137), kind=kLoop, calls=%fused_computation.85 | loop fusion | flops 1179648 | bytes 524289 | tf_op jit(solution)/shard_map/jit(_where)/select_n | solution.py:76
  28.1 0.0 all-gather.2.cloned.1.call-update
  28.2 0.7 convert_element_type.132
  28.9 0.9 convert_element_type.130
  29.8 0.7 add_select_fusion.2
  30.5 0.5 fusion.39
  31.0 0.7 fusion.69
  31.7 0.0 copy-start.1
  31.7 1.7 %fusion.17 = f32[1024,66]{0,1:T(8,128)S(1)} fusion(s32[1024]{0:T(1024)S(1)} %get-tuple-element.109, f32[1024,1]{0,1:T(1,128)S(1)} %bitcast.200, f32[1024,1]{0,1:T(1,128)S(1)} %bitcast.203, f32[1024,64]{0,1:T(8,128)S(1)} %convert_element_type.130), kind=kOutput, calls=%fused_computation.27 | convolution fusion | flops 831655936 | bytes 544768 | tf_op jit(solution)/shard_map/dot_general | solution.py:63
  33.4 0.1 copy.26
  33.5 0.1 copy.20
  33.6 0.0 copy-done.3
  33.6 0.8 pad_maximum_fusion
  34.4 15.2 %all-to-all-start.3 = ((f32[8,128,68]{1,2,0:T(8,128)}), f32[8,128,68]{1,2,0:T(8,128)S(1)}, u32[]{:S(2)}, u32[]{:S(2)}) async-start(f32[8,128,68]{1,2,0:T(8,128)} %pad_maximum_fusion), calls=%async_computation.3 | async-start | bytes 589824 | tf_op jit(solution)/shard_map/all_to_all | solution.py:67
  49.6 0.0 copy-done
  49.6 0.7 copy.23
  50.3 0.1 copy.24
  50.4 0.0 copy-done.1
  50.4 0.2 copy.22
  50.6 16.9 %all-to-all-done.3 = f32[8,128,68]{1,2,0:T(8,128)S(1)} async-done(((f32[8,128,68]{1,2,0:T(8,128)}), f32[8,128,68]{1,2,0:T(8,128)S(1)}, u32[]{:S(2)}, u32[]{:S(2)}) %all-to-all-start.3) | async-done | bytes 278560 | tf_op jit(solution)/shard_map/all_to_all | solution.py:67
  67.5 1.4 fusion.34
  68.9 0.6 convert_add_fusion
  70.2 0.1 copy.29
  70.3 0.1 copy.27
  70.4 6.2 %gather_fusion = s32[1024]{0:T(1024)S(1)} fusion(s32[2048]{0:T(1024)S(1)} %get-tuple-element.107, s32[1024]{0:T(1024)S(1)} %broadcast_clamp_fusion), kind=kCustom, calls=%fused_computation | custom fusion | bytes 12288 | tf_op jit(solution)/shard_map/jit(_take)/gather | solution.py:115
  76.6 1.4 fusion.35
  78.1 0.1 fusion.74
  78.1 0.1 fusion.75
  78.2 0.1 fusion.76
  78.3 26.7 %all-gather.2.cloned.1.call-done = bf16[4096,1024]{1,0:T(8,128)(2,1)} async-done(((bf16[128,1024]{1,0:T(8,128)(2,1)}), bf16[4096,1024]{1,0:T(8,128)(2,1)}) %all-gather.2.cloned.1.call-update) | async-done | bytes 8388624 | tf_op jit(solution)/shard_map/all_gather | solution.py:77
  105.0 9.8 %subtract_convert_fusion = bf16[128,1024]{1,0:T(8,128)(2,1)S(1)} fusion(s32[1024]{0:T(1024)S(1)} %bitcast.202, bf16[4096,1024]{1,0:T(8,128)(2,1)} %all-gather.2.cloned.1.call-done, bf16[128,4096]{0,1:T(8,128)(2,1)S(1)} %bitcast.124, bf16[128,1024]{0,1:T(8,128)(2,1)S(1)} %copy.22, f32[1024]{0:T(1024)S(1)} %bitcast.144, f32[1024]{0:T(1024)S(1)} %bitcast.145, ...), kind=kOutput, calls=%fused_computation.51 | convolution fusion | flops 1369178112 | bytes 10227712 | tf_op jit(solution)/shard_map/dot_general | solution.py:85
  114.8 45.2 %conditional.1 = (f32[32,128]{1,0:T(8,128)S(1)}) conditional(s32[]{:T(128)} %convert_element_type.140, (f32[1024,1]{0,1:T(1,128)S(1)}, bf16[128,1024]{1,0:T(8,128)(2,1)S(1)}, s32[256]{0:T(256)S(1)}) %tuple.90, (s32[1024]{0:T(1024)S(1)}, bf16[128,1024]{1,0:T(8,128)(2,1)S(1)}, bf16[32,304]{1,0:T(8,128)(2,1)S(1)}) %tuple.14), branch_computations={%region_3.6_spmd, %region_6.8_spmd} | conditional | flops 643526656 | bytes 3044364 | solution.py:141
  114.8 1.8 %fusion.13 = bf16[2432,128]{1,0:T(8,128)(2,1)S(1)} fusion(bf16[128,1024]{1,0:T(8,128)(2,1)S(1)} %get-tuple-element.26, s32[1024]{0:T(1024)S(1)} %get-tuple-element.25), kind=kOutput, calls=%fused_computation.16 | convolution fusion | flops 640335872 | bytes 888832 | tf_op jit(solution)/shard_map/cond/branch_1_fun/dot_general | solution.py:133
  116.6 43.1 %all_to_all.19 = bf16[8,304,128]{2,1,0:T(8,128)(2,1)S(1)} all-to-all(bf16[8,304,128]{2,1,0:T(8,128)(2,1)S(1)} %bitcast.128), channel_id=1, replica_groups=mesh['x'=4,'zh'=2,'y'=4,'c'=2,'trade'=8] {'trade'}, dimensions={0} | all-to-all | bytes 1245184 | tf_op jit(solution)/shard_map/cond/branch_1_fun/all_to_all | solution.py:137
  159.7 0.1 convert_reduce_fusion.1
  159.8 0.1 convolution_bitcast_fusion
  159.9 0.0 copy-start.2
  159.9 0.6 copy-done.2
  (13 shorter events, 0.2 us)
Async XLA Ops:
  6.5 27.0 %copy-start.3 = (s32[256]{0:T(256)S(1)}, s32[256]{0:T(256)}, u32[]{:S(2)}) copy-start(s32[256]{0:T(256)} %param.15) | copy-start | bytes 3076
  6.5 43.1 %copy-start = (bf16[128,4096]{1,0:T(8,128)(2,1)S(1)}, bf16[128,4096]{1,0:T(8,128)(2,1)}, u32[]{:S(2)}) copy-start(bf16[128,4096]{1,0:T(8,128)(2,1)} %param.9) | copy-start | bytes 3145732
  6.5 98.4 %all-gather.2.cloned.1.call-start = ((), (), s32[]{:S(2)}) async-start(), calls=%async_computation.4 | async-start | bytes 8650752 | tf_op jit(solution)/shard_map/all_gather | solution.py:77
  6.5 19.8 %collective-permute-start = (bf16[64,1024]{1,0:T(8,128)(2,1)}, bf16[64,1024]{1,0:T(8,128)(2,1)S(1)}, u32[]{:S(2)}, u32[]{:S(2)}) collective-permute-start(bf16[64,1024]{1,0:T(8,128)(2,1)} %param.10), channel_id=1, source_target_pairs={{0,64},{64,0},{1,65},{65,1},{2,66},{66,2},{3,67},{67,3},{4,68},{68... | collective-permute-start | bytes 393224 | tf_op jit(solution)/shard_map/ppermute | solution.py:74
  31.7 18.7 %copy-start.1 = (bf16[128,1024]{1,0:T(8,128)(2,1)S(1)}, bf16[128,1024]{1,0:T(8,128)(2,1)}, u32[]{:S(2)}) copy-start(bf16[128,1024]{1,0:T(8,128)(2,1)} %param.11) | copy-start | bytes 786436
  34.4 33.1 %all-to-all-start.3 = ((f32[8,128,68]{1,2,0:T(8,128)}), f32[8,128,68]{1,2,0:T(8,128)S(1)}, u32[]{:S(2)}, u32[]{:S(2)}) async-start(f32[8,128,68]{1,2,0:T(8,128)} %pad_maximum_fusion), calls=%async_computation.3 | async-start | bytes 589824 | tf_op jit(solution)/shard_map/all_to_all | solution.py:67
  159.9 0.6 copy-start.2
Sparse Core Ops, SparseCore 0:
  28.3 76.6 all-gather.1

commit v12 on v10

--- a/solution.py
+++ b/solution.py
@@ -122,12 +122,10 @@
         of_cp, at_slot, (((0,), (0,)), ((), ())), preferred_element_type=jnp.float32
     ).astype(jnp.bfloat16)
 
-    trade_slot, cp_table = lax.optimization_barrier((trade_slot, cp_table))
+    route = (trade_slot[None, :] == jnp.arange(owners * ROOM, dtype=jnp.int32)[:, None]).astype(jnp.bfloat16)
+    route, cp_table = lax.optimization_barrier((route, cp_table))
 
     def by_cp_owner(values):
-        route = (trade_slot[None, :] == jnp.arange(owners * ROOM, dtype=jnp.int32)[:, None]).astype(
-            jnp.bfloat16
-        )
         routed = lax.dot_general(
             route, values, (((1,), (1,)), ((), ())), preferred_element_type=jnp.float32
         )

time: 163 us -> 166 us (1.018)
  other arithmetic: 4.59 us -> 9.43 us
  waiting for transfers between devices: 43.4 us -> 38.6 us
  matrix products: 15.7 us -> 17.8 us
    convert_element_type x0 -> x1, other arithmetic: none -> 4.84 us  [per_device(): (trade_slot[None, :] == jnp.arange(owners * ROOM, dtype=jnp.int32)[:, Non...]
    all_gather x1, waiting for transfers between devices: 26.3 us -> 21.4 us  [per_device(): gathered = lax.all_gather(gathered, ('x', 'y', 'c'), axis=0, tiled=True)]
    dot_general x1, matrix products: 1.79 us -> 3.87 us  [by_cp_owner(): lax.dot_general(route, values, (((1,), (1,)), ((), ())), preferred_elemen...]
  transfers between devices with their start and end apart: 2 -> 2, of which waited for: 2 -> 2; matrix products, arithmetic and copies ran while one was open for 10% -> 13% of each run, Pallas kernels for 0% -> 0%
where the time goes in v12:
time: 166 us; the launch traced here: 165 us
  blocking collectives  63.4 us (38%)
  waiting for transfers between devices  38.6 us (23%)
  matrix products  17.8 us (11%)
  between operations  14.3 us (9%)
  starting transfers between devices  13.6 us (8%)
  other arithmetic  9.43 us (6%)
  local copies, waits for them, and re-layouts  7.99 us (5%)
    all_to_all x1, blocking collectives, by_cp_owner(): lax.all_to_all(sent, 'trade', 0, 0, tiled=False).astype(jnp.float32)  43.1 us
    all_gather x1, waiting for transfers between devices, per_device(): gathered = lax.all_gather(gathered, ('x', 'y', 'c'), axis=0, tiled=True)  21.4 us
    all_gather x1, blocking collectives, per_device(): gathered = lax.all_gather(loadings, 'zh', axis=0, tiled=True)  20.3 us
    all_to_all x1, waiting for transfers between devices, per_device(): got = lax.all_to_all(sent, 'trade', 0, 0, tiled=False)  17.1 us
    all_to_all x1, starting transfers between devices, per_device(): got = lax.all_to_all(sent, 'trade', 0, 0, tiled=False)  13.6 us
    dot_general x1, matrix products, per_device(): jnp.dot(factors, pick, preferred_element_type=jnp.float32)  8.72 us
    gather x1, local copies, waits for them, and re-layouts, per_device(): trade_slot = jnp.take(slot, got_ns)  6.15 us
    convert_element_type x1, other arithmetic, per_device(): (trade_slot[None, :] == jnp.arange(owners * ROOM, dtype=jnp.int32)[:, Non...  4.84 us
  transfers between devices with their start and end apart: 2, of which 2 were waited for; matrix products, arithmetic and copies ran while one was open for 13% of the time, Pallas kernels for 0%

profile of v12, /device:TPU:6, one launch (start us, length us, event | category | flops | bytes accessed | tf_op | source)
XLA Modules:
  0.0 165.0 jit_solution(17137452267530800110)
XLA Ops:
  6.5 0.0 copy-start.2
  6.5 0.0 copy-start
  6.5 0.0 all-gather.2.cloned.1.call-start
  6.5 20.3 %all_gather.6 = bf16[128,1024]{1,0:T(8,128)(2,1)} all-gather(bf16[64,1024]{1,0:T(8,128)(2,1)} %param.10), channel_id=1, replica_groups=mesh['x'=4,'zh'=2,'y'=4,'c'=2,'trade'=8] {'zh'}, dimensions={0}, use_global_device_ids=true | all-gather | bytes 393216 | tf_op jit(solution)/shard_map/all_gather | solution.py:74
  26.8 0.0 all-gather.2.cloned.1.call-update
  26.8 0.7 convert_element_type.134
  27.5 0.9 convert_element_type.132
  28.4 0.7 add_select_fusion.2
  29.1 0.5 fusion.36
  29.6 0.7 fusion.66
  30.3 1.7 %fusion.15 = f32[1024,66]{0,1:T(8,128)S(1)} fusion(s32[1024]{0:T(1024)S(1)} %get-tuple-element.109, f32[1024,1]{0,1:T(1,128)S(1)} %bitcast.191, f32[1024,1]{0,1:T(1,128)S(1)} %bitcast.194, f32[1024,64]{0,1:T(8,128)S(1)} %convert_element_type.132), kind=kOutput, calls=%fused_computation.26 | convolution fusion | flops 831655936 | bytes 544768 | tf_op jit(solution)/shard_map/dot_general | solution.py:63
  32.1 0.1 copy.25
  32.2 0.1 copy.20
  32.2 0.0 copy-done.2
  32.3 0.8 pad_maximum_fusion
  33.0 13.6 %all-to-all-start.3 = ((f32[8,128,68]{1,2,0:T(8,128)}), f32[8,128,68]{1,2,0:T(8,128)S(1)}, u32[]{:S(2)}, u32[]{:S(2)}) async-start(f32[8,128,68]{1,2,0:T(8,128)} %pad_maximum_fusion), calls=%async_computation.3 | async-start | bytes 589824 | tf_op jit(solution)/shard_map/all_to_all | solution.py:67
  46.6 0.0 copy-done
  46.6 0.7 copy.22
  47.2 0.1 copy.23
  47.3 17.1 %all-to-all-done.3 = f32[8,128,68]{1,2,0:T(8,128)S(1)} async-done(((f32[8,128,68]{1,2,0:T(8,128)}), f32[8,128,68]{1,2,0:T(8,128)S(1)}, u32[]{:S(2)}, u32[]{:S(2)}) %all-to-all-start.3) | async-done | bytes 278560 | tf_op jit(solution)/shard_map/all_to_all | solution.py:67
  64.5 1.4 fusion.31
  65.9 0.6 convert_add_fusion
  67.2 0.1 copy.28
  67.3 0.1 copy.26
  67.4 6.2 %gather_fusion = s32[1024]{0:T(1024)S(1)} fusion(s32[2048]{0:T(1024)S(1)} %get-tuple-element.107, s32[1024]{0:T(1024)S(1)} %broadcast_clamp_fusion), kind=kCustom, calls=%fused_computation | custom fusion | bytes 12288 | tf_op jit(solution)/shard_map/jit(_take)/gather | solution.py:113
  73.6 0.0 copy-start.3
  73.6 1.4 fusion.32
  75.0 4.8 %fusion.14 = bf16[2432,1024]{1,0:T(8,128)(2,1)} fusion(s32[1024]{0:T(1024)S(1)} %broadcast_select_fusion), kind=kLoop, calls=%fused_computation.22 | loop fusion | flops 4980736 | bytes 4984832 | tf_op jit(solution)/shard_map/convert_element_type | solution.py:125
  80.0 0.1 fusion.71
  80.0 0.1 fusion.72
  80.1 0.1 fusion.73
  80.2 21.4 %all-gather.2.cloned.1.call-done = bf16[4096,1024]{1,0:T(8,128)(2,1)} async-done(((bf16[128,1024]{1,0:T(8,128)(2,1)}), bf16[4096,1024]{1,0:T(8,128)(2,1)}) %all-gather.2.cloned.1.call-update) | async-done | bytes 8388624 | tf_op jit(solution)/shard_map/all_gather | solution.py:75
  101.6 0.0 copy-done.3
  101.6 8.7 %subtract_convert_fusion = bf16[128,1024]{1,0:T(8,128)(2,1)S(1)} fusion(s32[1024]{0:T(1024)S(1)} %bitcast.193, bf16[128,4096]{0,1:T(8,128)(2,1)S(1)} %bitcast.115, bf16[4096,1024]{1,0:T(8,128)(2,1)} %all-gather.2.cloned.1.call-done, bf16[128,1024]{1,0:T(8,128)(2,1)S(1)} %copy-done.3, f32[1024]{0:T(1024)S(1)} %bitcast.135, f32[1024]{0:T(1024)S(1)} %bitcast.136, ...), kind=kOutput, calls=%fused_computation.49 | convolution fusion | flops 1369178112 | bytes 10227712 | tf_op jit(solution)/shard_map/dot_general | solution.py:83
  110.3 47.3 %conditional.1 = (f32[32,128]{1,0:T(8,128)S(1)}) conditional(s32[]{:T(128)} %convert_element_type.142, (f32[1024,1]{0,1:T(1,128)S(1)}, bf16[128,1024]{1,0:T(8,128)(2,1)S(1)}, s32[256]{0:T(256)S(1)}) %tuple.90, (bf16[2432,1024]{1,0:T(8,128)(2,1)}, bf16[128,1024]{1,0:T(8,128)(2,1)S(1)}, bf16[32,304]{1,0:T(8,128)(2,1)S(1)}) %tuple.14), branch_computations={%region_3.6_spmd, %region_6.8_spmd} | conditional | flops 641036288 | bytes 7924744 | solution.py:137
  110.3 3.9 %convolution_convert_fusion = bf16[2432,128]{1,0:T(8,128)(2,1)S(1)} fusion(bf16[2432,1024]{1,0:T(8,128)(2,1)} %get-tuple-element.25, bf16[128,1024]{1,0:T(8,128)(2,1)S(1)} %get-tuple-element.26), kind=kOutput, calls=%fused_computation.13 | convolution fusion | flops 637845504 | bytes 5865472 | tf_op jit(solution)/shard_map/cond/branch_1_fun/dot_general | solution.py:129
  114.2 43.1 %all_to_all.19 = bf16[8,304,128]{2,1,0:T(8,128)(2,1)S(1)} all-to-all(bf16[8,304,128]{2,1,0:T(8,128)(2,1)S(1)} %bitcast.119), channel_id=1, replica_groups=mesh['x'=4,'zh'=2,'y'=4,'c'=2,'trade'=8] {'trade'}, dimensions={0} | all-to-all | bytes 1245184 | tf_op jit(solution)/shard_map/cond/branch_1_fun/all_to_all | solution.py:133
  157.4 0.1 convert_reduce_fusion.1
  157.4 0.1 convolution_bitcast_fusion
  157.6 0.0 copy-start.1
  157.6 0.6 copy-done.1
  (13 shorter events, 0.2 us)
Async XLA Ops:
  6.5 25.7 %copy-start.2 = (s32[256]{0:T(256)S(1)}, s32[256]{0:T(256)}, u32[]{:S(2)}) copy-start(s32[256]{0:T(256)} %param.15) | copy-start | bytes 3076
  6.5 40.0 %copy-start = (bf16[128,4096]{1,0:T(8,128)(2,1)S(1)}, bf16[128,4096]{1,0:T(8,128)(2,1)}, u32[]{:S(2)}) copy-start(bf16[128,4096]{1,0:T(8,128)(2,1)} %param.9) | copy-start | bytes 3145732
  6.5 95.1 %all-gather.2.cloned.1.call-start = ((), (), s32[]{:S(2)}) async-start(), calls=%async_computation.4 | async-start | bytes 8650752 | tf_op jit(solution)/shard_map/all_gather | solution.py:75
  33.0 31.5 %all-to-all-start.3 = ((f32[8,128,68]{1,2,0:T(8,128)}), f32[8,128,68]{1,2,0:T(8,128)S(1)}, u32[]{:S(2)}, u32[]{:S(2)}) async-start(f32[8,128,68]{1,2,0:T(8,128)} %pad_maximum_fusion), calls=%async_computation.3 | async-start | bytes 589824 | tf_op jit(solution)/shard_map/all_to_all | solution.py:67
  73.6 28.0 %copy-start.3 = (bf16[128,1024]{1,0:T(8,128)(2,1)S(1)}, bf16[128,1024]{1,0:T(8,128)(2,1)}, u32[]{:S(2)}) copy-start(bf16[128,1024]{1,0:T(8,128)(2,1)} %param.11) | copy-start | bytes 786436
  157.6 0.6 copy-start.1
Sparse Core Ops, SparseCore 0:
  26.9 74.6 all-gather.1

commit v13 on v10

--- a/solution.py
+++ b/solution.py
@@ -4,7 +4,7 @@
 from jax.sharding import Mesh, PartitionSpec as P
 
 CP_DEV = 32
-ROOM = 304
+ROOM = 296
 
 
 def clenshaw(chosen, coeffs_t):

time: 163 us -> 163 us (level)
  no operation moved by 1% of the time
where the time goes in v13:
time: 163 us; the launch traced here: 162 us
  blocking collectives  62.7 us (38%)
  waiting for transfers between devices  43.4 us (27%)
  matrix products  15.7 us (10%)
  between operations  14.3 us (9%)
  starting transfers between devices  13.6 us (8%)
  local copies, waits for them, and re-layouts  7.98 us (5%)
  other arithmetic  4.59 us (3%)
    all_to_all x1, blocking collectives, by_cp_owner(): lax.all_to_all(sent, 'trade', 0, 0, tiled=False).astype(jnp.float32)  42.4 us
    all_gather x1, waiting for transfers between devices, per_device(): gathered = lax.all_gather(gathered, ('x', 'y', 'c'), axis=0, tiled=True)  26.3 us
    all_gather x1, blocking collectives, per_device(): gathered = lax.all_gather(loadings, 'zh', axis=0, tiled=True)  20.3 us
    all_to_all x1, waiting for transfers between devices, per_device(): got = lax.all_to_all(sent, 'trade', 0, 0, tiled=False)  17.1 us
    all_to_all x1, starting transfers between devices, per_device(): got = lax.all_to_all(sent, 'trade', 0, 0, tiled=False)  13.6 us
    dot_general x1, matrix products, per_device(): jnp.dot(factors, pick, preferred_element_type=jnp.float32)  8.73 us
    gather x1, local copies, waits for them, and re-layouts, per_device(): trade_slot = jnp.take(slot, got_ns)  6.15 us
  transfers between devices with their start and end apart: 2, of which 2 were waited for; matrix products, arithmetic and copies ran while one was open for 10% of the time, Pallas kernels for 0%

profile of v13, /device:TPU:6, one launch (start us, length us, event | category | flops | bytes accessed | tf_op | source)
XLA Modules:
  0.0 162.2 jit_solution(14877389387775387609)
XLA Ops:
  6.5 0.0 copy-start.2
  6.5 0.0 copy-start
  6.5 0.0 all-gather.2.cloned.1.call-start
  6.5 20.3 %all_gather.6 = bf16[128,1024]{1,0:T(8,128)(2,1)} all-gather(bf16[64,1024]{1,0:T(8,128)(2,1)} %param.10), channel_id=1, replica_groups=mesh['x'=4,'zh'=2,'y'=4,'c'=2,'trade'=8] {'zh'}, dimensions={0}, use_global_device_ids=true | all-gather | bytes 393216 | tf_op jit(solution)/shard_map/all_gather | solution.py:74
  26.8 0.0 all-gather.2.cloned.1.call-update
  26.8 0.7 convert_element_type.132
  27.5 0.9 convert_element_type.130
  28.4 0.7 add_select_fusion.2
  29.1 0.5 fusion.38
  29.6 0.7 fusion.68
  30.3 1.7 %fusion.17 = f32[1024,66]{0,1:T(8,128)S(1)} fusion(s32[1024]{0:T(1024)S(1)} %get-tuple-element.109, f32[1024,1]{0,1:T(1,128)S(1)} %bitcast.190, f32[1024,1]{0,1:T(1,128)S(1)} %bitcast.193, f32[1024,64]{0,1:T(8,128)S(1)} %convert_element_type.130), kind=kOutput, calls=%fused_computation.27 | convolution fusion | flops 831655936 | bytes 544768 | tf_op jit(solution)/shard_map/dot_general | solution.py:63
  32.1 0.1 copy.25
  32.2 0.1 copy.20
  32.2 0.0 copy-done.2
  32.3 0.8 pad_maximum_fusion
  33.0 13.6 %all-to-all-start.3 = ((f32[8,128,68]{1,2,0:T(8,128)}), f32[8,128,68]{1,2,0:T(8,128)S(1)}, u32[]{:S(2)}, u32[]{:S(2)}) async-start(f32[8,128,68]{1,2,0:T(8,128)} %pad_maximum_fusion), calls=%async_computation.3 | async-start | bytes 589824 | tf_op jit(solution)/shard_map/all_to_all | solution.py:67
  46.6 0.0 copy-done
  46.6 0.7 copy.22
  47.2 0.1 copy.23
  47.3 17.1 %all-to-all-done.3 = f32[8,128,68]{1,2,0:T(8,128)S(1)} async-done(((f32[8,128,68]{1,2,0:T(8,128)}), f32[8,128,68]{1,2,0:T(8,128)S(1)}, u32[]{:S(2)}, u32[]{:S(2)}) %all-to-all-start.3) | async-done | bytes 278560 | tf_op jit(solution)/shard_map/all_to_all | solution.py:67
  64.5 1.4 fusion.33
  65.9 0.6 convert_add_fusion
  67.2 0.1 copy.28
  67.3 0.0 copy-start.3
  67.3 0.1 copy.26
  67.4 6.2 %gather_fusion = s32[1024]{0:T(1024)S(1)} fusion(s32[2048]{0:T(1024)S(1)} %get-tuple-element.107, s32[1024]{0:T(1024)S(1)} %broadcast_clamp_fusion), kind=kCustom, calls=%fused_computation | custom fusion | bytes 12288 | tf_op jit(solution)/shard_map/jit(_take)/gather | solution.py:113
  73.6 1.4 fusion.34
  75.1 0.1 fusion.73
  75.2 0.1 fusion.74
  75.3 0.1 fusion.75
  75.3 26.3 %all-gather.2.cloned.1.call-done = bf16[4096,1024]{1,0:T(8,128)(2,1)} async-done(((bf16[128,1024]{1,0:T(8,128)(2,1)}), bf16[4096,1024]{1,0:T(8,128)(2,1)}) %all-gather.2.cloned.1.call-update) | async-done | bytes 8388624 | tf_op jit(solution)/shard_map/all_gather | solution.py:75
  101.6 0.0 copy-done.3
  101.6 8.7 %subtract_convert_fusion = bf16[128,1024]{1,0:T(8,128)(2,1)S(1)} fusion(s32[1024]{0:T(1024)S(1)} %bitcast.192, bf16[128,4096]{0,1:T(8,128)(2,1)S(1)} %bitcast.114, bf16[4096,1024]{1,0:T(8,128)(2,1)} %all-gather.2.cloned.1.call-done, bf16[128,1024]{1,0:T(8,128)(2,1)S(1)} %copy-done.3, f32[1024]{0:T(1024)S(1)} %bitcast.134, f32[1024]{0:T(1024)S(1)} %bitcast.135, ...), kind=kOutput, calls=%fused_computation.50 | convolution fusion | flops 1369178112 | bytes 10227712 | tf_op jit(solution)/shard_map/dot_general | solution.py:83
  110.3 44.4 %conditional.1 = (f32[32,128]{1,0:T(8,128)S(1)}) conditional(s32[]{:T(128)} %convert_element_type.140, (f32[1024,1]{0,1:T(1,128)S(1)}, bf16[128,1024]{1,0:T(8,128)(2,1)S(1)}, s32[256]{0:T(256)S(1)}) %tuple.90, (s32[1024]{0:T(1024)S(1)}, bf16[128,1024]{1,0:T(8,128)(2,1)S(1)}, bf16[32,296]{1,0:T(8,128)(2,1)S(1)}) %tuple.14), branch_computations={%region_3.6_spmd, %region_6.8_spmd} | conditional | flops 626591744 | bytes 3044364 | solution.py:139
  110.4 1.7 %fusion.13 = bf16[2368,128]{1,0:T(8,128)(2,1)S(1)} fusion(bf16[128,1024]{1,0:T(8,128)(2,1)S(1)} %get-tuple-element.26, s32[1024]{0:T(1024)S(1)} %get-tuple-element.25), kind=kOutput, calls=%fused_computation.16 | convolution fusion | flops 623484928 | bytes 872448 | tf_op jit(solution)/shard_map/cond/branch_1_fun/dot_general | solution.py:131
  112.1 42.4 %all_to_all.19 = bf16[8,296,128]{2,1,0:T(8,128)(2,1)S(1)} all-to-all(bf16[8,296,128]{2,1,0:T(8,128)(2,1)S(1)} %bitcast.118), channel_id=1, replica_groups=mesh['x'=4,'zh'=2,'y'=4,'c'=2,'trade'=8] {'trade'}, dimensions={0} | all-to-all | bytes 1212416 | tf_op jit(solution)/shard_map/cond/branch_1_fun/all_to_all | solution.py:135
  154.5 0.1 convert_reduce_fusion.1
  154.6 0.1 convolution_bitcast_fusion
  154.8 0.0 copy-start.1
  154.8 0.6 copy-done.1
  (13 shorter events, 0.2 us)
Async XLA Ops:
  6.5 25.7 %copy-start.2 = (s32[256]{0:T(256)S(1)}, s32[256]{0:T(256)}, u32[]{:S(2)}) copy-start(s32[256]{0:T(256)} %param.15) | copy-start | bytes 3076
  6.5 40.0 %copy-start = (bf16[128,4096]{1,0:T(8,128)(2,1)S(1)}, bf16[128,4096]{1,0:T(8,128)(2,1)}, u32[]{:S(2)}) copy-start(bf16[128,4096]{1,0:T(8,128)(2,1)} %param.9) | copy-start | bytes 3145732
  6.5 95.1 %all-gather.2.cloned.1.call-start = ((), (), s32[]{:S(2)}) async-start(), calls=%async_computation.4 | async-start | bytes 8650752 | tf_op jit(solution)/shard_map/all_gather | solution.py:75
  33.0 31.5 %all-to-all-start.3 = ((f32[8,128,68]{1,2,0:T(8,128)}), f32[8,128,68]{1,2,0:T(8,128)S(1)}, u32[]{:S(2)}, u32[]{:S(2)}) async-start(f32[8,128,68]{1,2,0:T(8,128)} %pad_maximum_fusion), calls=%async_computation.3 | async-start | bytes 589824 | tf_op jit(solution)/shard_map/all_to_all | solution.py:67
  67.3 34.3 %copy-start.3 = (bf16[128,1024]{1,0:T(8,128)(2,1)S(1)}, bf16[128,1024]{1,0:T(8,128)(2,1)}, u32[]{:S(2)}) copy-start(bf16[128,1024]{1,0:T(8,128)(2,1)} %param.11) | copy-start | bytes 786436
  154.8 0.6 copy-start.1
Sparse Core Ops, SparseCore 0:
  26.9 74.6 all-gather.1
